TPU v7x, 1024 devices: a whole 8x8x8 slice. The times are simulated.
1024 devices in a mesh: dp: 8 (over x), seq: 8 (over z), enc: 16 (over y, core).
Axes of the slice: x: 8, y: 8, z: 8, core: 2. Of those that a mesh axis runs over, the one named last changes fastest.
Arguments:
- queries: bfloat16 [128, 1024, 2048], P(('dp', 'enc'), 'seq'), may hold values from -12 to 12
- cotangent: bfloat16 [128, 1024, 2048], P(('dp', 'enc'), 'seq'), may hold values from -12 to 12
- key_pool: bfloat16 [8, 8, 8, 128, 2048], P('dp', 'seq', None, None, 'enc'), may hold values from -12 to 12
- value_pool: bfloat16 [8, 8, 8, 128, 2048], P('dp', 'seq', None, None, 'enc'), may hold values from -6 to 6
- counts: int32 [128, 16], P('dp', 'seq'), may hold values from 0 to 4
- neighbour_ids: int32 [128, 16, 4], P('dp', 'seq'), may hold values from 0 to 7, all different within a row
- rel_bias: float32 [16, 191], P('enc'), may hold values from -3 to 3
Outputs:
- context: bfloat16 [128, 1024, 2048], P(('dp', 'enc'), 'seq')
- query_grad: bfloat16 [128, 1024, 2048], P(('dp', 'enc'), 'seq')
- key_grad: bfloat16 [8, 8, 8, 128, 2048], P('dp', 'seq', None, None, 'enc')
- value_grad: bfloat16 [8, 8, 8, 128, 2048], P('dp', 'seq', None, None, 'enc')
- bias_grad: float32 [16, 191], P('enc')
Inputs may be any that keep to these rules, and one draw needn't show every extreme that they name: Only the first counts[c] ids of a block are used. `neighbour_ids`: the 4 ids of one block are distinct.
All inputs are finite; a program needn't handle non-finite values.
Results may differ from a plain program's by a relative error of at most 0.0085.
Values may be sent and summed in bfloat16 or wider, within the bound.
No kernel may reach another device: no remote copies, remote signals or barrier semaphores. Data moves between devices by JAX's collectives and lax.ppermute only.
A program may use at most 64 MiB of HBM per device.

v0:
```python
import math

import jax
import jax.numpy as jnp
from jax import lax
from jax.sharding import PartitionSpec as P

HEAD_DIM = 128
BLOCK_LEN = 64
PASSAGE = 128


NEG_FILL = -1e30


def bias_rows(bias_table):
    heads_here, table_width = bias_table.shape
    padded = jnp.pad(bias_table, ((0, 0), (0, 1)))
    tiled_rows = jnp.broadcast_to(padded[:, None, :], (heads_here, BLOCK_LEN, table_width + 1))
    tiled_rows = tiled_rows.reshape(heads_here, BLOCK_LEN * (table_width + 1))[
        :, : BLOCK_LEN * table_width
    ]
    tiled_rows = tiled_rows.reshape(heads_here, BLOCK_LEN, table_width)
    return tiled_rows[:, :, BLOCK_LEN - 1 : BLOCK_LEN - 1 + PASSAGE]


def fold_bias(totals, table_width):
    heads_here = totals.shape[0]
    padded = jnp.pad(totals, ((0, 0), (0, 0), (BLOCK_LEN - 1, 0)))
    flat_rows = padded.reshape(heads_here, BLOCK_LEN * table_width)
    flat_rows = jnp.pad(flat_rows, ((0, 0), (0, BLOCK_LEN)))
    return flat_rows.reshape(heads_here, BLOCK_LEN, table_width + 1).sum(axis=1)[:, :table_width]


def forward_pass(query_heads, id_table, count_table, pool_keys, pool_values, row_bias):
    score_scale = 1.0 / math.sqrt(HEAD_DIM)
    block_total = query_heads.shape[0]
    batch_blocks = 8
    batch_count = block_total // batch_blocks

    def forward_one_batch(pieces):
        query_block, id_block, count_block = pieces
        keys_sel = pool_keys[id_block]
        values_sel = pool_values[id_block]
        scores = (
            jnp.einsum(
                "cqhd,cjthd->chqjt", query_block, keys_sel, preferred_element_type=jnp.float32
            )
            * score_scale
        )
        scores = scores + row_bias[None, :, :, None, :]
        slot_index = jnp.arange(id_block.shape[1])
        usable = (slot_index[None, :] < count_block[:, None])[:, None, None, :, None]
        row_top = jnp.max(jnp.where(usable, scores, NEG_FILL), axis=(3, 4), keepdims=True)
        raised = jnp.where(usable, jnp.exp(scores - row_top), 0.0)
        no_keys = (count_block == 0).astype(jnp.float32)[:, None, None, None, None]
        weights = raised / (jnp.sum(raised, axis=(3, 4), keepdims=True) + no_keys)
        context_block = jnp.einsum(
            "chqjt,cjthd->cqhd",
            weights.astype(jnp.bfloat16),
            values_sel,
            preferred_element_type=jnp.float32,
        )
        return (context_block.astype(jnp.bfloat16), weights)

    context_blocks, weight_blocks = lax.map(
        forward_one_batch,
        (
            query_heads.reshape((batch_count, batch_blocks) + query_heads.shape[1:]),
            id_table.reshape(batch_count, batch_blocks, id_table.shape[1]),
            count_table.reshape(batch_count, batch_blocks),
        ),
    )
    return (context_blocks.reshape(query_heads.shape), weight_blocks)


def backward_pass(query_heads, grad_heads, weight_blocks, id_table, pool_keys, pool_values):
    score_scale = 1.0 / math.sqrt(HEAD_DIM)
    batch_count, batch_blocks = (weight_blocks.shape[0], weight_blocks.shape[1])
    pool_size = pool_keys.shape[0]
    heads_here = pool_keys.shape[2]

    def backward_one_batch(running, pieces):
        key_total, value_total, bias_total = running
        query_block, grad_block, weights, id_block = pieces
        keys_sel = pool_keys[id_block]
        values_sel = pool_values[id_block]
        grad_weights = jnp.einsum(
            "cqhd,cjthd->chqjt", grad_block, values_sel, preferred_element_type=jnp.float32
        )
        row_delta = jnp.sum(weights * grad_weights, axis=(3, 4), keepdims=True)
        grad_scores = weights * (grad_weights - row_delta)
        scores_low = grad_scores.astype(jnp.bfloat16)
        weights_low = weights.astype(jnp.bfloat16)
        query_block_grad = score_scale * jnp.einsum(
            "chqjt,cjthd->cqhd", scores_low, keys_sel, preferred_element_type=jnp.float32
        )
        key_slots = jnp.einsum(
            "chqjt,cqhd->cjthd", scores_low, query_block, preferred_element_type=jnp.float32
        )
        value_slots = jnp.einsum(
            "chqjt,cqhd->cjthd", weights_low, grad_block, preferred_element_type=jnp.float32
        )
        flat_ids = id_block.reshape(-1)
        key_total = key_total.at[flat_ids].add(key_slots.reshape((-1,) + key_slots.shape[2:]))
        value_total = value_total.at[flat_ids].add(
            value_slots.reshape((-1,) + value_slots.shape[2:])
        )
        bias_total = bias_total + jnp.sum(grad_scores, axis=(0, 3))
        return ((key_total, value_total, bias_total), query_block_grad.astype(jnp.bfloat16))

    pool_zeros = jnp.zeros((pool_size, PASSAGE, heads_here, HEAD_DIM), jnp.float32)
    bias_zeros = jnp.zeros((heads_here, BLOCK_LEN, PASSAGE), jnp.float32)
    running, query_grads = lax.scan(
        backward_one_batch,
        (pool_zeros, pool_zeros, bias_zeros),
        (
            query_heads.reshape((batch_count, batch_blocks) + query_heads.shape[1:]),
            grad_heads.reshape((batch_count, batch_blocks) + grad_heads.shape[1:]),
            weight_blocks,
            id_table.reshape(batch_count, batch_blocks, id_table.shape[1]),
        ),
    )
    key_total, value_total, bias_total = running
    return (
        query_grads.reshape(query_heads.shape),
        score_scale * key_total,
        value_total,
        bias_total,
    )


def local(queries, cotangent, key_pool, value_pool, counts, neighbour_ids, rel_bias):
    token_rows = queries.shape[1]
    full_width = queries.shape[2]
    blocks_here = token_rows // BLOCK_LEN
    head_width = key_pool.shape[-1]
    heads_here = head_width // HEAD_DIM
    pool_size = key_pool.shape[2]
    pool_keys = key_pool.reshape(pool_size, PASSAGE, heads_here, HEAD_DIM)
    pool_values = value_pool.reshape(pool_size, PASSAGE, heads_here, HEAD_DIM)
    id_table = neighbour_ids.reshape(-1, neighbour_ids.shape[-1])
    count_table = counts.reshape(-1)
    row_bias = bias_rows(rel_bias)
    query_rows = queries.reshape(blocks_here, BLOCK_LEN, full_width)
    grad_rows = cotangent.reshape(blocks_here, BLOCK_LEN, full_width)

    def to_heads(moved_rows):
        return moved_rows.reshape(moved_rows.shape[0], BLOCK_LEN, heads_here, HEAD_DIM)

    def to_rows(head_rows):
        return head_rows.reshape(head_rows.shape[0], BLOCK_LEN, head_width)

    query_heads = to_heads(
        lax.all_to_all(query_rows, "enc", split_axis=2, concat_axis=0, tiled=True)
    )
    context_heads, weight_blocks = forward_pass(
        query_heads, id_table, count_table, pool_keys, pool_values, row_bias
    )
    context_rows = lax.all_to_all(
        to_rows(context_heads), "enc", split_axis=0, concat_axis=2, tiled=True
    )
    grad_heads = to_heads(lax.all_to_all(grad_rows, "enc", split_axis=2, concat_axis=0, tiled=True))
    query_part, key_total, value_total, bias_total = backward_pass(
        query_heads, grad_heads, weight_blocks, id_table, pool_keys, pool_values
    )
    query_back = lax.all_to_all(to_rows(query_part), "enc", split_axis=0, concat_axis=2, tiled=True)
    bias_grad = lax.psum(fold_bias(bias_total, rel_bias.shape[1]), ("dp", "seq"))
    return (
        context_rows.reshape(queries.shape),
        query_back.reshape(queries.shape),
        key_total.astype(jnp.bfloat16).reshape(key_pool.shape),
        value_total.astype(jnp.bfloat16).reshape(value_pool.shape),
        bias_grad,
    )


def solution(mesh):
    in_specs = (
        P(("dp", "enc"), "seq", None),
        P(("dp", "enc"), "seq", None),
        P("dp", "seq", None, None, "enc"),
        P("dp", "seq", None, None, "enc"),
        P("dp", "seq"),
        P("dp", "seq", None),
        P("enc", None),
    )
    out_specs = (
        P(("dp", "enc"), "seq", None),
        P(("dp", "enc"), "seq", None),
        P("dp", "seq", None, None, "enc"),
        P("dp", "seq", None, None, "enc"),
        P("enc", None),
    )
    return jax.shard_map(local, mesh=mesh, in_specs=in_specs, out_specs=out_specs, check_vma=False)
```

profile of v0, /device:TPU:32, one launch (start us, length us, event | category | flops | bytes accessed | tf_op | source)
XLA Modules:
  0.0 348.8 jit_solution(8324258176828163641)
XLA Ops:
  4.6 16.1 %all-to-all-start = ((bf16[16,2,8192]{2,1,0:T(2,128)(2,1)}), bf16[16,2,8192]{2,1,0:T(2,128)(2,1)S(1)}, u32[]{:S(2)}, u32[]{:S(2)}) async-start(bf16[16,2,8192]{2,1,0:T(2,128)(2,1)} %reshape.408), calls=%async_computation | async-start | bytes 1048576 | tf_op jit(solution)/shard_map/all_to_all | solution.py:155
  23.9 11.8 %all-to-all-done = bf16[16,2,8192]{2,1,0:T(2,128)(2,1)S(1)} async-done(((bf16[16,2,8192]{2,1,0:T(2,128)(2,1)}), bf16[16,2,8192]{2,1,0:T(2,128)(2,1)S(1)}, u32[]{:S(2)}, u32[]{:S(2)}) %all-to-all-start) | async-done | bytes 524320 | tf_op jit(solution)/shard_map/all_to_all | solution.py:155
  35.7 5.3 %all-to-all-start.2 = ((bf16[16,2,8192]{2,1,0:T(2,128)(2,1)}), bf16[16,2,8192]{2,1,0:T(2,128)(2,1)S(1)}, u32[]{:S(2)}, u32[]{:S(2)}) async-start(bf16[16,2,8192]{2,1,0:T(2,128)(2,1)} %reshape.410), calls=%async_computation.2 | async-start | bytes 1048576 | tf_op jit(solution)/shard_map/all_to_all | solution.py:163
  44.4 24.6 %while.29 = (s32[]{:T(128)}, bf16[4,8,64,1,128]{4,2,1,3,0:T(8,128)(2,1)}, f32[4,8,1,64,4,128]{5,3,4,1,2,0:T(8,128)}, s32[4,8,4]{1,2,0:T(4,128)S(1)}, bf16[8,128,...) while((s32[]{:T(128)}, ...), condition=%wide.region_3.4_spmd, body=%wide.region_0.3_spmd.sunk | while | flops 137953936 | bytes 11853377 | solution.py:66
  69.0 7.2 %all-to-all-start.1 = ((bf16[32,64,128]{2,1,0:T(8,128)(2,1)}), bf16[32,64,128]{2,1,0:T(8,128)(2,1)}, u32[]{:S(2)}, u32[]{:S(2)}) async-start(bf16[32,64,128]{2,1,0:T(8,128)(2,1)} %bitcast.259), calls=%async_computation.1 | async-start | bytes 1048576 | tf_op jit(solution)/shard_map/all_to_all | solution.py:160
  79.6 109.0 %while.30 = (s32[]{:T(128)}, f32[8,128,1,128]{3,1,0,2:T(8,128)S(1)}, f32[8,128,1,128]{3,1,0,2:T(8,128)S(1)}, f32[1,64,128]{2,1,0:T(8,128)S(1)}, bf16[4,8,64,1,12...) while((s32[]{:T(128)}, ...), condition=%wide.region_9.10_spmd.clone, body=%wide.region_4.9_spmd.clone.sunk | while | flops 271196864 | bytes 38416796 | solution.py:114
  84.1 2.7 fusion.72
  86.9 2.9 copy.103
  89.8 4.7 %scatter_fusion = f32[8,128,128]{2,1,0:T(8,128)S(1)} fusion(f32[8,128,128]{2,1,0:T(8,128)S(1)} %bitcast.243, s32[32]{0:T(128)S(1)} %fusion.69, f32[32,128,128]{2,1,0:T(8,128)} %copy.103), kind=kCustom, calls=%fused_computation.4.clone.clone.1 | custom fusion | flops 524288 | bytes 6291584 | tf_op jit(solution)/shard_map/while/body/eval_jaxpr/scatter-add | solution.py:105
  94.4 3.1 fusion.73
  97.5 2.9 copy.104
  100.5 4.7 %scatter_fusion.1 = f32[8,128,128]{2,1,0:T(8,128)S(1)} fusion(f32[8,128,128]{2,1,0:T(8,128)S(1)} %bitcast.245, s32[32]{0:T(128)S(1)} %fusion.69, f32[32,128,128]{2,1,0:T(8,128)} %copy.104), kind=kCustom, calls=%fused_computation.5.clone.clone.1 | custom fusion | flops 524288 | bytes 6291584 | tf_op jit(solution)/shard_map/while/body/eval_jaxpr/scatter-add | solution.py:106
  111.4 2.7 fusion.72
  114.1 2.9 copy.103
  117.0 4.7 %scatter_fusion = f32[8,128,128]{2,1,0:T(8,128)S(1)} fusion(f32[8,128,128]{2,1,0:T(8,128)S(1)} %bitcast.243, s32[32]{0:T(128)S(1)} %fusion.69, f32[32,128,128]{2,1,0:T(8,128)} %copy.103), kind=kCustom, calls=%fused_computation.4.clone.clone.1 | custom fusion | flops 524288 | bytes 6291584 | tf_op jit(solution)/shard_map/while/body/eval_jaxpr/scatter-add | solution.py:105
  121.7 3.1 fusion.73
  124.8 2.9 copy.104
  127.7 4.7 %scatter_fusion.1 = f32[8,128,128]{2,1,0:T(8,128)S(1)} fusion(f32[8,128,128]{2,1,0:T(8,128)S(1)} %bitcast.245, s32[32]{0:T(128)S(1)} %fusion.69, f32[32,128,128]{2,1,0:T(8,128)} %copy.104), kind=kCustom, calls=%fused_computation.5.clone.clone.1 | custom fusion | flops 524288 | bytes 6291584 | tf_op jit(solution)/shard_map/while/body/eval_jaxpr/scatter-add | solution.py:106
  138.6 2.7 fusion.72
  141.3 2.9 copy.103
  144.2 4.7 %scatter_fusion = f32[8,128,128]{2,1,0:T(8,128)S(1)} fusion(f32[8,128,128]{2,1,0:T(8,128)S(1)} %bitcast.243, s32[32]{0:T(128)S(1)} %fusion.69, f32[32,128,128]{2,1,0:T(8,128)} %copy.103), kind=kCustom, calls=%fused_computation.4.clone.clone.1 | custom fusion | flops 524288 | bytes 6291584 | tf_op jit(solution)/shard_map/while/body/eval_jaxpr/scatter-add | solution.py:105
  148.9 3.1 fusion.73
  152.0 2.9 copy.104
  154.9 4.7 %scatter_fusion.1 = f32[8,128,128]{2,1,0:T(8,128)S(1)} fusion(f32[8,128,128]{2,1,0:T(8,128)S(1)} %bitcast.245, s32[32]{0:T(128)S(1)} %fusion.69, f32[32,128,128]{2,1,0:T(8,128)} %copy.104), kind=kCustom, calls=%fused_computation.5.clone.clone.1 | custom fusion | flops 524288 | bytes 6291584 | tf_op jit(solution)/shard_map/while/body/eval_jaxpr/scatter-add | solution.py:106
  165.9 2.7 fusion.72
  168.6 2.9 copy.103
  171.5 4.7 %scatter_fusion = f32[8,128,128]{2,1,0:T(8,128)S(1)} fusion(f32[8,128,128]{2,1,0:T(8,128)S(1)} %bitcast.243, s32[32]{0:T(128)S(1)} %fusion.69, f32[32,128,128]{2,1,0:T(8,128)} %copy.103), kind=kCustom, calls=%fused_computation.4.clone.clone.1 | custom fusion | flops 524288 | bytes 6291584 | tf_op jit(solution)/shard_map/while/body/eval_jaxpr/scatter-add | solution.py:105
  176.2 3.1 fusion.73
  179.3 2.9 copy.104
  182.2 4.7 %scatter_fusion.1 = f32[8,128,128]{2,1,0:T(8,128)S(1)} fusion(f32[8,128,128]{2,1,0:T(8,128)S(1)} %bitcast.245, s32[32]{0:T(128)S(1)} %fusion.69, f32[32,128,128]{2,1,0:T(8,128)} %copy.104), kind=kCustom, calls=%fused_computation.5.clone.clone.1 | custom fusion | flops 524288 | bytes 6291584 | tf_op jit(solution)/shard_map/while/body/eval_jaxpr/scatter-add | solution.py:106
  188.6 7.2 %all-to-all-start.3 = ((bf16[32,64,128]{2,1,0:T(8,128)(2,1)}), bf16[32,64,128]{2,1,0:T(8,128)(2,1)S(1)}, u32[]{:S(2)}, u32[]{:S(2)}) async-start(bf16[32,64,128]{2,1,0:T(8,128)(2,1)} %bitcast.258), calls=%async_computation.3 | async-start | bytes 1048576 | tf_op jit(solution)/shard_map/all_to_all | solution.py:167
  196.4 147.7 %psum.7 = f32[1,191]{1,0:T(1,128)} all-reduce(f32[1,191]{1,0:T(1,128)S(1)} %bitcast.264), channel_id=1, replica_groups=mesh['dp'=8,'seq'=8,'enc'=16] {'dp','seq'}, use_global_device_ids=true, to_apply=%region_11.12 | all-reduce | flops 191 | bytes 1528 | tf_op jit(solution)/shard_map/psum | solution.py:168
  (153 shorter events, 68.4 us)
Async XLA Ops:
  0.6 20.1 %copy-start.3 = (s32[16,2,4]{0,2,1:T(4,128)S(1)}, s32[16,2,4]{0,2,1:T(4,128)}, u32[]{:S(2)}) copy-start(s32[16,2,4]{0,2,1:T(4,128)} %param.16) | copy-start | bytes 1540
  0.6 20.3 %copy-start.4 = (s32[16,2]{0,1:T(2,128)S(1)}, s32[16,2]{0,1:T(2,128)}, u32[]{:S(2)}) copy-start(s32[16,2]{0,1:T(2,128)} %param.15) | copy-start | bytes 388
  0.7 20.5 %copy-start.5 = (f32[1,191]{1,0:T(1,128)S(1)}, f32[1,191]{1,0:T(1,128)}, u32[]{:S(2)}) copy-start(f32[1,191]{1,0:T(1,128)} %param.17) | copy-start | bytes 2296
  0.7 21.0 %copy-start.2 = (bf16[1,128,2048]{2,1,0:T(8,128)(2,1)S(1)}, bf16[1,128,2048]{2,1,0:T(8,128)(2,1)}, u32[]{:S(2)}) copy-start(bf16[1,128,2048]{2,1,0:T(8,128)(2,1)} %param.12) | copy-start | bytes 1572868
  4.6 31.1 %all-to-all-start = ((bf16[16,2,8192]{2,1,0:T(2,128)(2,1)}), bf16[16,2,8192]{2,1,0:T(2,128)(2,1)S(1)}, u32[]{:S(2)}, u32[]{:S(2)}) async-start(bf16[16,2,8192]{2,1,0:T(2,128)(2,1)} %reshape.408), calls=%async_computation | async-start | bytes 1048576 | tf_op jit(solution)/shard_map/all_to_all | solution.py:155
  35.7 33.3 %all-to-all-start.2 = ((bf16[16,2,8192]{2,1,0:T(2,128)(2,1)}), bf16[16,2,8192]{2,1,0:T(2,128)(2,1)S(1)}, u32[]{:S(2)}, u32[]{:S(2)}) async-start(bf16[16,2,8192]{2,1,0:T(2,128)(2,1)} %reshape.410), calls=%async_computation.2 | async-start | bytes 1048576 | tf_op jit(solution)/shard_map/all_to_all | solution.py:163
  41.0 3.4 copy-start
  41.0 3.4 copy-start.1
  69.0 119.6 %all-to-all-start.1 = ((bf16[32,64,128]{2,1,0:T(8,128)(2,1)}), bf16[32,64,128]{2,1,0:T(8,128)(2,1)}, u32[]{:S(2)}, u32[]{:S(2)}) async-start(bf16[32,64,128]{2,1,0:T(8,128)(2,1)} %bitcast.259), calls=%async_computation.1 | async-start | bytes 1048576 | tf_op jit(solution)/shard_map/all_to_all | solution.py:160
  188.6 158.8 %all-to-all-start.3 = ((bf16[32,64,128]{2,1,0:T(8,128)(2,1)}), bf16[32,64,128]{2,1,0:T(8,128)(2,1)S(1)}, u32[]{:S(2)}, u32[]{:S(2)}) async-start(bf16[32,64,128]{2,1,0:T(8,128)(2,1)} %bitcast.258), calls=%async_computation.3 | async-start | bytes 1048576 | tf_op jit(solution)/shard_map/all_to_all | solution.py:167
where the time goes:
time: 351 us; the launch traced here: 349 us
  blocking collectives  148 us (42%)
  local copies, waits for them, and re-layouts  55.4 us (16%)
  other arithmetic  51.9 us (15%)
  matrix products  45 us (13%)
  starting transfers between devices  35.9 us (10%)
  waiting for transfers between devices  11.8 us (3%)
    psum x1, blocking collectives, local(): lax.psum(fold_bias(bias_total, rel_bias.shape[1]), ('dp', 'seq'))  148 us
    scatter-add x4, other arithmetic, backward_one_batch(): key_total.at[flat_ids].add(key_slots.reshape((-1,) + key_slots.shape[2:]))  18.6 us
    scatter-add x4, other arithmetic, backward_one_batch(): value_total.at[flat_ids]  18.6 us
    all_to_all x1, starting transfers between devices, local(): lax.all_to_all(query_rows, 'enc', split_axis=2, concat_axis=0, tiled=True)  16.1 us
    dot_general x4, matrix products, backward_one_batch(): jnp.einsum('chqjt,cqhd->cjthd', weights_low, grad_block, preferred_elemen...  12.5 us
    all_to_all x1, waiting for transfers between devices, local(): lax.all_to_all(query_rows, 'enc', split_axis=2, concat_axis=0, tiled=True)  11.8 us
    reshape x4, local copies, waits for them, and re-layouts, backward_one_batch(): value_slots.reshape((-1,) + value_slots.shape[2:])  11.6 us
    reshape x4, local copies, waits for them, and re-layouts, backward_one_batch(): key_slots.reshape((-1,) + key_slots.shape[2:])  11.6 us
  transfers between devices with their start and end apart: 4, of which 1 were waited for; matrix products, arithmetic and copies ran while one was open for 42% of the time, Pallas kernels for 0%

commit v1 on v0

v1 whole, which is shorter than its diff:
```python
import math

import jax
import jax.numpy as jnp
from jax import lax
from jax.sharding import PartitionSpec as P

HEAD_DIM = 128
BLOCK_LEN = 64
PASSAGE = 128


NEG_FILL = -1e30


def bias_rows(bias_table):
    heads_here, table_width = bias_table.shape
    padded = jnp.pad(bias_table, ((0, 0), (0, 1)))
    tiled_rows = jnp.broadcast_to(padded[:, None, :], (heads_here, BLOCK_LEN, table_width + 1))
    tiled_rows = tiled_rows.reshape(heads_here, BLOCK_LEN * (table_width + 1))[
        :, : BLOCK_LEN * table_width
    ]
    tiled_rows = tiled_rows.reshape(heads_here, BLOCK_LEN, table_width)
    return tiled_rows[:, :, BLOCK_LEN - 1 : BLOCK_LEN - 1 + PASSAGE]


def fold_bias(totals, table_width):
    heads_here = totals.shape[0]
    padded = jnp.pad(totals, ((0, 0), (0, 0), (BLOCK_LEN - 1, 0)))
    flat_rows = padded.reshape(heads_here, BLOCK_LEN * table_width)
    flat_rows = jnp.pad(flat_rows, ((0, 0), (0, BLOCK_LEN)))
    return flat_rows.reshape(heads_here, BLOCK_LEN, table_width + 1).sum(axis=1)[:, :table_width]


def attend_all(query_heads, grad_heads, id_table, count_table, pool_keys, pool_values, row_bias):
    score_scale = 1.0 / math.sqrt(HEAD_DIM)
    pool_size = pool_keys.shape[0]
    width = pool_size * PASSAGE
    keys_flat = pool_keys.reshape(width, HEAD_DIM)
    values_flat = pool_values.reshape(width, HEAD_DIM)
    slot_index = jnp.arange(id_table.shape[1])
    picked = (slot_index[None, :] < count_table[:, None])[:, :, None] & (
        id_table[:, :, None] == jnp.arange(pool_size)[None, None, :]
    )
    usable = jnp.repeat(jnp.any(picked, axis=1), PASSAGE, axis=1)[:, None, :]
    bias_wide = jnp.tile(row_bias[0], (1, pool_size))[None]
    scores = (
        jnp.einsum("cqd,kd->cqk", query_heads, keys_flat, preferred_element_type=jnp.float32)
        * score_scale
    )
    scores = scores + bias_wide
    row_top = jnp.max(jnp.where(usable, scores, NEG_FILL), axis=2, keepdims=True)
    raised = jnp.where(usable, jnp.exp(scores - row_top), 0.0)
    no_keys = (count_table == 0).astype(jnp.float32)[:, None, None]
    weights = raised / (jnp.sum(raised, axis=2, keepdims=True) + no_keys)
    weights_low = weights.astype(jnp.bfloat16)
    context = jnp.einsum(
        "cqk,kd->cqd", weights_low, values_flat, preferred_element_type=jnp.float32
    ).astype(jnp.bfloat16)
    grad_weights = jnp.einsum(
        "cqd,kd->cqk", grad_heads, values_flat, preferred_element_type=jnp.float32
    )
    row_delta = jnp.sum(weights * grad_weights, axis=2, keepdims=True)
    grad_scores = weights * (grad_weights - row_delta)
    scores_low = grad_scores.astype(jnp.bfloat16)
    query_grad = (
        score_scale
        * jnp.einsum("cqk,kd->cqd", scores_low, keys_flat, preferred_element_type=jnp.float32)
    ).astype(jnp.bfloat16)
    key_grad = score_scale * jnp.einsum(
        "cqk,cqd->kd", scores_low, query_heads, preferred_element_type=jnp.float32
    )
    value_grad = jnp.einsum(
        "cqk,cqd->kd", weights_low, grad_heads, preferred_element_type=jnp.float32
    )
    bias_total = jnp.sum(grad_scores, axis=0).reshape(BLOCK_LEN, pool_size, PASSAGE).sum(axis=1)
    return (context, query_grad, key_grad, value_grad, bias_total[None])


def reduce_groups(part):
    return lax.psum(lax.psum(part, "dp"), "seq")


def local(queries, cotangent, key_pool, value_pool, counts, neighbour_ids, rel_bias):
    token_rows = queries.shape[1]
    full_width = queries.shape[2]
    blocks_here = token_rows // BLOCK_LEN
    head_width = key_pool.shape[-1]
    heads_here = head_width // HEAD_DIM
    pool_size = key_pool.shape[2]
    pool_keys = key_pool.reshape(pool_size, PASSAGE, head_width)
    pool_values = value_pool.reshape(pool_size, PASSAGE, head_width)
    id_table = neighbour_ids.reshape(-1, neighbour_ids.shape[-1])
    count_table = counts.reshape(-1)
    row_bias = bias_rows(rel_bias)
    both_rows = jnp.stack(
        [
            queries.reshape(blocks_here, BLOCK_LEN, full_width),
            cotangent.reshape(blocks_here, BLOCK_LEN, full_width),
        ]
    )
    both_heads = lax.all_to_all(both_rows, "enc", split_axis=3, concat_axis=1, tiled=True)
    context_heads, query_part, key_total, value_total, bias_total = attend_all(
        both_heads[0], both_heads[1], id_table, count_table, pool_keys, pool_values, row_bias
    )
    both_back = lax.all_to_all(
        jnp.stack([context_heads, query_part]), "enc", split_axis=1, concat_axis=3, tiled=True
    )
    bias_grad = reduce_groups(fold_bias(bias_total, rel_bias.shape[1]))
    return (
        both_back[0].reshape(queries.shape),
        both_back[1].reshape(queries.shape),
        key_total.astype(jnp.bfloat16).reshape(key_pool.shape),
        value_total.astype(jnp.bfloat16).reshape(value_pool.shape),
        bias_grad,
    )


def solution(mesh):
    in_specs = (
        P(("dp", "enc"), "seq", None),
        P(("dp", "enc"), "seq", None),
        P("dp", "seq", None, None, "enc"),
        P("dp", "seq", None, None, "enc"),
        P("dp", "seq"),
        P("dp", "seq", None),
        P("enc", None),
    )
    out_specs = (
        P(("dp", "enc"), "seq", None),
        P(("dp", "enc"), "seq", None),
        P("dp", "seq", None, None, "enc"),
        P("dp", "seq", None, None, "enc"),
        P("enc", None),
    )
    return jax.shard_map(local, mesh=mesh, in_specs=in_specs, out_specs=out_specs, check_vma=False)
```

time: 351 us -> 133 us (0.38)
  the two profiles are of different devices: /device:TPU:32 before, /device:TPU:16 now
where the time goes in v1:
time: 133 us
  blocking collectives  38.5 us (29%)
  matrix products  26.4 us (20%)
  starting transfers between devices  23.2 us (17%)
  waiting for transfers between devices  22.8 us (17%)
  local copies, waits for them, and re-layouts  17.6 us (13%)
  other arithmetic  3.32 us (2%)
    psum x2, blocking collectives, reduce_groups(): return lax.psum(lax.psum(part, 'dp'), 'seq')  38.5 us
    all_to_all x1, waiting for transfers between devices, local(): lax.all_to_all(both_rows, 'enc', split_axis=3, concat_axis=1, tiled=True)  22.8 us
    all_to_all x1, starting transfers between devices, local(): lax.all_to_all(both_rows, 'enc', split_axis=3, concat_axis=1, tiled=True)  16.4 us
    sub x1, matrix products, attend_all(): raised = jnp.where(usable, jnp.exp(scores - row_top), 0.0)  8.16 us
    unnamed x21, local copies, waits for them, and re-layouts  7.51 us
    all_to_all x1, starting transfers between devices, local(): lax.all_to_all(jnp.stack([context_heads, query_part]), 'enc', split_axis=...  6.77 us
    dot_general x1, matrix products, attend_all(): jnp.einsum('cqk,cqd->kd', weights_low, grad_heads, preferred_element_type...  5.8 us
    dot_general x1, matrix products, attend_all(): jnp.einsum('cqk,kd->cqd', weights_low, values_flat, preferred_element_typ...  4.84 us
  transfers between devices with their start and end apart: 2, of which 1 were waited for; matrix products, arithmetic and copies ran while one was open for 9% of the time, Pallas kernels for 0%

profile of v1, /device:TPU:16, one launch (start us, length us, event | category | flops | bytes accessed | tf_op | source)
XLA Modules:
  0.0 132.7 jit_solution(2833065075328621027)
XLA Ops:
  0.7 1.3 %pad_maximum_fusion = bf16[2,2,64,2048]{3,2,1,0:T(8,128)(2,1)S(1)} fusion(bf16[1,2,64,2048]{3,2,1,0:T(8,128)(2,1)} %bitcast.79, bf16[1,2,64,2048]{3,2,1,0:T(8,128)(2,1)} %bitcast.80), kind=kLoop, calls=%fused_computation.29 | loop fusion | flops 524288 | bytes 2097152 | tf_op jit(solution)/shard_map/stack | solution.py:96
  2.0 1.5 %copy.45 = bf16[2,2,64,2048]{2,1,0,3:T(2,128)(2,1)S(1)} copy(bf16[2,2,64,2048]{3,2,1,0:T(8,128)(2,1)S(1)} %pad_maximum_fusion) | data formatting | bytes 2097152 | tf_op jit(solution)/shard_map/stack | solution.py:96
  3.6 2.3 %reshape.127 = bf16[16,2,16384]{2,1,0:T(2,128)(2,1)} reshape(bf16[2048,2,2,64]{3,2,1,0:T(2,128)(2,1)S(1)} %bitcast.69) | data formatting | bytes 2097152
  5.8 16.4 %all-to-all-start = ((bf16[16,2,16384]{2,1,0:T(2,128)(2,1)}), bf16[16,2,16384]{2,1,0:T(2,128)(2,1)S(1)}, u32[]{:S(2)}, u32[]{:S(2)}) async-start(bf16[16,2,16384]{2,1,0:T(2,128)(2,1)} %reshape.127), calls=%async_computation | async-start | bytes 2097152 | tf_op jit(solution)/shard_map/all_to_all | solution.py:102
  23.0 0.1 slice_reduce_fusion
  23.2 0.2 reshape.105
  23.5 0.8 copy.58
  24.2 22.8 %all-to-all-done = bf16[16,2,16384]{2,1,0:T(2,128)(2,1)S(1)} async-done(((bf16[16,2,16384]{2,1,0:T(2,128)(2,1)}), bf16[16,2,16384]{2,1,0:T(2,128)(2,1)S(1)}, u32[]{:S(2)}, u32[]{:S(2)}) %all-to-all-start) | async-done | bytes 1048608 | tf_op jit(solution)/shard_map/all_to_all | solution.py:102
  47.0 1.3 %reshape.128 = bf16[2048,2,2,64]{3,2,1,0:T(2,128)(2,1)S(1)} reshape(bf16[16,2,16384]{2,1,0:T(2,128)(2,1)S(1)} %all-to-all-done) | data formatting | bytes 2097152
  48.4 2.7 %copy.52 = bf16[2,2,64,16,128]{4,3,2,1,0:T(8,128)(2,1)S(1)} copy(bf16[2,2,64,16,128]{2,1,0,4,3:T(2,128)(2,1)S(1)} %bitcast.70) | data formatting | bytes 2097152 | tf_op jit(solution)/shard_map/all_to_all | solution.py:102
  51.1 0.2 fusion.37
  51.2 0.1 copy.47
  51.4 0.1 copy.48
  51.5 8.2 %fusion.38 = (f32[32,64]{1,0:T(8,128)S(1)}, f32[32,64,1024]{2,1,0:T(8,128)}) fusion(f32[64,1024]{1,0:T(8,128)} %bitcast.81, pred[32,1024]{1,0:T(8,128)(4,1)S(1)} %bitcast.85, bf16[32,64,128]{2,1,0:T(8,128)(2,1)S(1)} %bitcast.75, bf16[1024,128,1]{1,0,2:T(8,128)(2,1)} %bitcast.88), kind=kOutput, calls=%fused_computation.47 | convolution fusion | flops 1090520064 | bytes 9478144 | tf_op jit(solution)/shard_map/sub | solution.py:53
  59.8 4.8 %fusion.19 = bf16[1,32,64,128]{3,2,1,0:T(8,128)(2,1)S(1)} fusion(bf16[1024,128,1]{1,0,2:T(8,128)(2,1)S(1)} %bitcast.67, f32[32,64,1024]{2,1,0:T(8,128)} %get-tuple-element.12, f32[32,64]{1,0:T(8,128)S(1)} %broadcast_add_fusion), kind=kOutput, calls=%fused_computation.22 | convolution fusion | flops 541327360 | bytes 9183232 | tf_op jit(solution)/shard_map/cqk,kd->cqd/dot_general | solution.py:57
  64.6 0.9 copy-done.1
  65.5 2.1 %multiply_reduce_fusion = (f32[32,64]{1,0:T(8,128)S(1)}, f32[32,64,1024]{2,1,0:T(8,128)S(1)}) fusion(f32[32,64,1024]{2,1,0:T(8,128)S(1)} %copy-done.1, f32[32,64]{1,0:T(8,128)S(1)} %broadcast_add_fusion, bf16[32,64,128]{2,1,0:T(8,128)(2,1)S(1)} %bitcast.77, bf16[1024,128,1]{1,0,2:T(8,128)(2,1)S(1)} %bitcast.68), kind=kOutput, calls=%fused_computation.2 | convolution fusion | flops 543160320 | bytes 17580032 | tf_op jit(solution)/shard_map/cqd,kd->cqk/dot_general | solution.py:60
  67.7 1.7 %fusion.8 = (f32[64,1024]{1,0:T(8,128)S(1)}, bf16[32,64,1024]{2,1,0:T(8,128)(2,1)S(1)}) fusion(f32[32,64,1024]{2,1,0:T(8,128)S(1)} %get-tuple-element.14, f32[32,64]{1,0:T(8,128)S(1)} %get-tuple-element.13, f32[32,64,1024]{2,1,0:T(8,128)S(1)} %copy-done.1, f32[32,64]{1,0:T(8,128)S(1)} %broadcast_add_fusion), kind=kLoop, calls=%fused_computation.12 | loop fusion | flops 10420224 | bytes 21250048 | tf_op jit(solution)/shard_map/reduce_sum | solution.py:76
  69.4 2.0 %copy-done.2 = bf16[32,64,1024]{2,1,0:T(8,128)(2,1)} copy-done((bf16[32,64,1024]{2,1,0:T(8,128)(2,1)}, bf16[32,64,1024]{2,1,0:T(8,128)(2,1)S(1)}, u32[]{:S(2)}) %copy-start.2) | copy-done | bytes 4194328
  71.3 1.3 fusion.18
  72.8 1.1 copy.49
  73.9 6.8 %all-to-all-start.1 = ((bf16[2,32,64,128]{3,2,0,1:T(8,128)(2,1)}), bf16[2,32,64,128]{3,2,0,1:T(8,128)(2,1)S(1)}, u32[]{:S(2)}, u32[]{:S(2)}) async-start(bf16[2,32,64,128]{3,2,0,1:T(8,128)(2,1)} %copy.49), calls=%async_computation.1 | async-start | bytes 2097152 | tf_op jit(solution)/shard_map/all_to_all | solution.py:106
  80.9 0.3 reshape.109
  81.1 0.1 pad_reduce_fusion
  81.4 14.2 %psum.14 = f32[1,191]{1,0:T(1,128)S(1)} all-reduce(f32[1,191]{1,0:T(1,128)S(1)} %bitcast.86), channel_id=1, replica_groups=mesh['dp'=8,'seq'=8,'enc'=16] {'dp'}, use_global_device_ids=true, to_apply=%region_7.8 | all-reduce | flops 191 | bytes 1528 | tf_op jit(solution)/shard_map/psum | solution.py:81
  95.5 24.4 %psum.15 = f32[1,191]{1,0:T(1,128)} all-reduce(f32[1,191]{1,0:T(1,128)S(1)} %psum.14), channel_id=1, replica_groups=mesh['dp'=8,'seq'=8,'enc'=16] {'seq'}, use_global_device_ids=true, to_apply=%region_8.9 | all-reduce | flops 191 | bytes 1528 | tf_op jit(solution)/shard_map/psum | solution.py:81
  119.9 4.2 %fusion.28 = bf16[1024,128]{1,0:T(8,128)(2,1)} fusion(bf16[32,64,1024]{2,1,0:T(8,128)(2,1)} %copy-done.2, bf16[32,64,128]{2,1,0:T(8,128)(2,1)S(1)} %bitcast.76), kind=kOutput, calls=%fused_computation.27 | convolution fusion | flops 537133056 | bytes 4980736 | tf_op jit(solution)/shard_map/cqk,cqd->kd/dot_general | solution.py:70
  124.1 5.8 %fusion.29 = bf16[1024,128]{1,0:T(8,128)(2,1)} fusion(bf16[32,64,128]{2,1,0:T(8,128)(2,1)S(1)} %bitcast.78, f32[32,64,1024]{2,1,0:T(8,128)} %get-tuple-element.12, f32[32,64]{1,0:T(8,128)S(1)} %broadcast_add_fusion), kind=kOutput, calls=%fused_computation.28 | convolution fusion | flops 541196288 | bytes 9183232 | tf_op jit(solution)/shard_map/cqk,cqd->kd/dot_general | solution.py:73
  130.0 0.3 copy.50
  130.3 1.0 reshape_squeeze.6
  131.4 0.3 copy.51
  131.7 1.0 reshape_squeeze.7
  (36 shorter events, 1.4 us)
Async XLA Ops:
  0.6 59.1 %copy-start = (bf16[1,1,8,128,128]{4,3,2,1,0:T(8,128)(2,1)S(1)}, bf16[1,1,8,128,128]{4,3,2,1,0:T(8,128)(2,1)}, u32[]{:S(2)}) copy-start(bf16[1,1,8,128,128]{4,3,2,1,0:T(8,128)(2,1)} %param.10) | copy-start | bytes 786436
  0.6 21.6 %copy-start.4 = (s32[16,2]{0,1:T(2,128)S(1)}, s32[16,2]{0,1:T(2,128)}, u32[]{:S(2)}) copy-start(s32[16,2]{0,1:T(2,128)} %param.11) | copy-start | bytes 388
  0.7 21.8 %copy-start.3 = (s32[16,2,4]{0,2,1:T(4,128)S(1)}, s32[16,2,4]{0,2,1:T(4,128)}, u32[]{:S(2)}) copy-start(s32[16,2,4]{0,2,1:T(4,128)} %param.12) | copy-start | bytes 1540
  0.7 22.2 %copy-start.5 = (f32[1,191]{1,0:T(1,128)S(1)}, f32[1,191]{1,0:T(1,128)}, u32[]{:S(2)}) copy-start(f32[1,191]{1,0:T(1,128)} %param.13) | copy-start | bytes 2296
  5.8 41.2 %all-to-all-start = ((bf16[16,2,16384]{2,1,0:T(2,128)(2,1)}), bf16[16,2,16384]{2,1,0:T(2,128)(2,1)S(1)}, u32[]{:S(2)}, u32[]{:S(2)}) async-start(bf16[16,2,16384]{2,1,0:T(2,128)(2,1)} %reshape.127), calls=%async_computation | async-start | bytes 2097152 | tf_op jit(solution)/shard_map/all_to_all | solution.py:102
  59.8 5.8 %copy-start.1 = (f32[32,64,1024]{2,1,0:T(8,128)S(1)}, f32[32,64,1024]{2,1,0:T(8,128)}, u32[]{:S(2)}) copy-start(f32[32,64,1024]{2,1,0:T(8,128)} %get-tuple-element.12) | copy-start | bytes 25165828
  67.6 3.7 %copy-start.6 = (bf16[1,1,8,128,128]{4,3,2,1,0:T(8,128)(2,1)S(1)}, bf16[1,1,8,128,128]{4,3,2,1,0:T(8,128)(2,1)}, u32[]{:S(2)}) copy-start(bf16[1,1,8,128,128]{4,3,2,1,0:T(8,128)(2,1)} %param.9) | copy-start | bytes 786436
  69.4 2.0 %copy-start.2 = (bf16[32,64,1024]{2,1,0:T(8,128)(2,1)}, bf16[32,64,1024]{2,1,0:T(8,128)(2,1)S(1)}, u32[]{:S(2)}) copy-start(bf16[32,64,1024]{2,1,0:T(8,128)(2,1)S(1)} %get-tuple-element.6) | copy-start | bytes 12582916
  73.9 56.0 %all-to-all-start.1 = ((bf16[2,32,64,128]{3,2,0,1:T(8,128)(2,1)}), bf16[2,32,64,128]{3,2,0,1:T(8,128)(2,1)S(1)}, u32[]{:S(2)}, u32[]{:S(2)}) async-start(bf16[2,32,64,128]{3,2,0,1:T(8,128)(2,1)} %copy.49), calls=%async_computation.1 | async-start | bytes 2097152 | tf_op jit(solution)/shard_map/all_to_all | solution.py:106

commit v2 on v1

v2 whole, which is shorter than its diff:
```python
import math

import jax
import jax.numpy as jnp
from jax import lax
from jax.experimental import pallas as pl
from jax.experimental.pallas import tpu as pltpu
from jax.sharding import PartitionSpec as P

HEAD_DIM = 128
BLOCK_LEN = 64
PASSAGE = 128


NEG_FILL = -1e30


def bias_rows(bias_table):
    heads_here, table_width = bias_table.shape
    padded = jnp.pad(bias_table, ((0, 0), (0, 1)))
    tiled_rows = jnp.broadcast_to(padded[:, None, :], (heads_here, BLOCK_LEN, table_width + 1))
    tiled_rows = tiled_rows.reshape(heads_here, BLOCK_LEN * (table_width + 1))[
        :, : BLOCK_LEN * table_width
    ]
    tiled_rows = tiled_rows.reshape(heads_here, BLOCK_LEN, table_width)
    return tiled_rows[:, :, BLOCK_LEN - 1 : BLOCK_LEN - 1 + PASSAGE]


def fold_bias(totals, table_width):
    heads_here = totals.shape[0]
    padded = jnp.pad(totals, ((0, 0), (0, 0), (BLOCK_LEN - 1, 0)))
    flat_rows = padded.reshape(heads_here, BLOCK_LEN * table_width)
    flat_rows = jnp.pad(flat_rows, ((0, 0), (0, BLOCK_LEN)))
    return flat_rows.reshape(heads_here, BLOCK_LEN, table_width + 1).sum(axis=1)[:, :table_width]


def attend_kernel(qd_ref, keys_ref, values_ref, bias_ref, mask_ref, out_ref, key_out, value_out,
                  bias_out, key_acc, value_acc, bias_acc):
    step = pl.program_id(0)
    score_scale = 1.0 / math.sqrt(HEAD_DIM)
    seqs_here, halves, rows_seq, _ = qd_ref.shape
    blocks_seq = rows_seq // BLOCK_LEN
    rows = seqs_here * rows_seq
    width = keys_ref.shape[0]
    tile4 = (seqs_here, blocks_seq, BLOCK_LEN, width)
    contract_last = (((1,), (1,)), ((), ()))
    contract_first = (((0,), (0,)), ((), ()))

    @pl.when(step == 0)
    def _():
        key_acc[...] = jnp.zeros_like(key_acc)
        value_acc[...] = jnp.zeros_like(value_acc)
        bias_acc[...] = jnp.zeros_like(bias_acc)

    query_rows = qd_ref[:, 0].reshape(rows, HEAD_DIM)
    grad_rows = qd_ref[:, 1].reshape(rows, HEAD_DIM)
    keys = keys_ref[...]
    values = values_ref[...]
    scores = lax.dot_general(query_rows, keys, contract_last, preferred_element_type=jnp.float32)
    scores = scores.reshape(tile4) * score_scale + bias_ref[...][None, None]
    usable = mask_ref[...][:, :, None, :] > 0.5
    row_top = jnp.max(jnp.where(usable, scores, NEG_FILL), axis=3, keepdims=True)
    raised = jnp.where(usable, jnp.exp(scores - row_top), 0.0)
    total = jnp.sum(raised, axis=3, keepdims=True)
    weights = raised / (total + jnp.where(total == 0.0, 1.0, 0.0))
    weights_low = weights.astype(jnp.bfloat16).reshape(rows, width)
    context = jnp.dot(weights_low, values, preferred_element_type=jnp.float32)
    grad_weights = lax.dot_general(grad_rows, values, contract_last, preferred_element_type=jnp.float32)
    grad_weights = grad_weights.reshape(tile4)
    row_delta = jnp.sum(weights * grad_weights, axis=3, keepdims=True)
    grad_scores = weights * (grad_weights - row_delta)
    scores_low = grad_scores.astype(jnp.bfloat16).reshape(rows, width)
    query_grad = score_scale * jnp.dot(scores_low, keys, preferred_element_type=jnp.float32)
    out_ref[:, 0] = context.astype(jnp.bfloat16).reshape(seqs_here, rows_seq, HEAD_DIM)
    out_ref[:, 1] = query_grad.astype(jnp.bfloat16).reshape(seqs_here, rows_seq, HEAD_DIM)
    key_acc[...] += lax.dot_general(scores_low, query_rows, contract_first, preferred_element_type=jnp.float32)
    value_acc[...] += lax.dot_general(weights_low, grad_rows, contract_first, preferred_element_type=jnp.float32)
    bias_acc[...] += jnp.sum(grad_scores, axis=(0, 1))

    @pl.when(step == pl.num_programs(0) - 1)
    def _():
        key_out[...] = (score_scale * key_acc[...]).astype(key_out.dtype)
        value_out[...] = value_acc[...].astype(value_out.dtype)
        folded = bias_acc[:, 0:PASSAGE]
        for part in range(1, width // PASSAGE):
            folded = folded + bias_acc[:, part * PASSAGE:(part + 1) * PASSAGE]
        bias_out[...] = folded


def attend_all(both_heads, id_table, count_table, pool_keys, pool_values, row_bias):
    seq_total, halves, rows_seq, _ = both_heads.shape
    pool_size = pool_keys.shape[0]
    width = pool_size * PASSAGE
    blocks_seq = rows_seq // BLOCK_LEN
    keys_flat = pool_keys.reshape(width, HEAD_DIM)
    values_flat = pool_values.reshape(width, HEAD_DIM)
    slot_index = jnp.arange(id_table.shape[1])
    picked = (slot_index[None, :] < count_table[:, None])[:, :, None] & (
        id_table[:, :, None] == jnp.arange(pool_size)[None, None, :]
    )
    usable = jnp.repeat(jnp.any(picked, axis=1).astype(jnp.float32), PASSAGE, axis=1)
    usable = usable.reshape(seq_total, blocks_seq, width)
    bias_wide = jnp.tile(row_bias[0], (1, pool_size))
    seqs_step = 2
    grid = (seq_total // seqs_step,)
    return pl.pallas_call(
        attend_kernel,
        grid=grid,
        in_specs=[
            pl.BlockSpec((seqs_step, halves, rows_seq, HEAD_DIM), lambda i: (i, 0, 0, 0)),
            pl.BlockSpec((width, HEAD_DIM), lambda i: (0, 0)),
            pl.BlockSpec((width, HEAD_DIM), lambda i: (0, 0)),
            pl.BlockSpec((BLOCK_LEN, width), lambda i: (0, 0)),
            pl.BlockSpec((seqs_step, blocks_seq, width), lambda i: (i, 0, 0)),
        ],
        out_specs=[
            pl.BlockSpec((seqs_step, halves, rows_seq, HEAD_DIM), lambda i: (i, 0, 0, 0)),
            pl.BlockSpec((width, HEAD_DIM), lambda i: (0, 0)),
            pl.BlockSpec((width, HEAD_DIM), lambda i: (0, 0)),
            pl.BlockSpec((BLOCK_LEN, PASSAGE), lambda i: (0, 0)),
        ],
        out_shape=[
            jax.ShapeDtypeStruct(both_heads.shape, jnp.bfloat16),
            jax.ShapeDtypeStruct((width, HEAD_DIM), jnp.bfloat16),
            jax.ShapeDtypeStruct((width, HEAD_DIM), jnp.bfloat16),
            jax.ShapeDtypeStruct((BLOCK_LEN, PASSAGE), jnp.float32),
        ],
        scratch_shapes=[
            pltpu.VMEM((width, HEAD_DIM), jnp.float32),
            pltpu.VMEM((width, HEAD_DIM), jnp.float32),
            pltpu.VMEM((BLOCK_LEN, width), jnp.float32),
        ],
        compiler_params=pltpu.CompilerParams(dimension_semantics=("arbitrary",)),
    )(both_heads, keys_flat, values_flat, bias_wide, usable)


def reduce_groups(part):
    return lax.psum(lax.psum(part, "dp"), "seq")


def local(queries, cotangent, key_pool, value_pool, counts, neighbour_ids, rel_bias):
    token_rows = queries.shape[1]
    full_width = queries.shape[2]
    blocks_here = token_rows // BLOCK_LEN
    head_width = key_pool.shape[-1]
    heads_total = full_width // HEAD_DIM
    pool_size = key_pool.shape[2]
    pool_keys = key_pool.reshape(pool_size, PASSAGE, head_width)
    pool_values = value_pool.reshape(pool_size, PASSAGE, head_width)
    id_table = neighbour_ids.reshape(-1, neighbour_ids.shape[-1])
    count_table = counts.reshape(-1)
    row_bias = bias_rows(rel_bias)
    both_rows = jnp.stack(
        [
            queries.reshape(token_rows, heads_total, HEAD_DIM),
            cotangent.reshape(token_rows, heads_total, HEAD_DIM),
        ]
    ).transpose(2, 0, 1, 3)
    both_heads = lax.all_to_all(both_rows, "enc", split_axis=0, concat_axis=0, tiled=True)
    both_out, key_total, value_total, bias_total = attend_all(
        both_heads, id_table, count_table, pool_keys, pool_values, row_bias
    )
    both_back = lax.all_to_all(both_out, "enc", split_axis=0, concat_axis=0, tiled=True)
    both_back = both_back.transpose(1, 2, 0, 3).reshape((2,) + queries.shape)
    bias_grad = reduce_groups(fold_bias(bias_total[None], rel_bias.shape[1]))
    return (
        both_back[0],
        both_back[1],
        key_total.reshape(key_pool.shape),
        value_total.reshape(value_pool.shape),
        bias_grad,
    )


def solution(mesh):
    in_specs = (
        P(("dp", "enc"), "seq", None),
        P(("dp", "enc"), "seq", None),
        P("dp", "seq", None, None, "enc"),
        P("dp", "seq", None, None, "enc"),
        P("dp", "seq"),
        P("dp", "seq", None),
        P("enc", None),
    )
    out_specs = (
        P(("dp", "enc"), "seq", None),
        P(("dp", "enc"), "seq", None),
        P("dp", "seq", None, None, "enc"),
        P("dp", "seq", None, None, "enc"),
        P("enc", None),
    )
    return jax.shard_map(local, mesh=mesh, in_specs=in_specs, out_specs=out_specs, check_vma=False)
```

time: 133 us -> 111 us (0.83)
  matrix products: 26.4 us -> 0 us
  Pallas kernels: 0 us -> 15.4 us
  local copies, waits for them, and re-layouts: 17.6 us -> 10.8 us
  other arithmetic: 3.32 us -> 1.14 us
  waiting for transfers between devices: 22.8 us -> 21 us
    dot_general x5 -> x0, matrix products: 18.2 us -> none  [the longest x1 5.8 us: attend_all(): jnp.einsum('cqk,cqd->kd', weights_low, grad_heads, preferred_element_type...]
    pallas_call x0 -> x1, Pallas kernels: none -> 15.4 us  [attend_all(): pl.pallas_call(attend_kernel, grid=grid, in_specs=[pl.BlockSpec((seqs_ste...]
    sub x1 -> x0, matrix products: 8.16 us -> none  [attend_all(): raised = jnp.where(usable, jnp.exp(scores - row_top), 0.0)]
    another operation x6 -> x5, local copies, waits for them, and re-layouts: 4.82 us -> 1.38 us  [the longest x1 0.73 us: attend_all(): usable = usable.reshape(seq_total, blocks_seq, width)]
    all_to_all x1 -> x0, local copies, waits for them, and re-layouts: 2.68 us -> none  [local(): lax.all_to_all(both_rows, 'enc', split_axis=3, concat_axis=1, tiled=True)]
    all_to_all x2, waiting for transfers between devices: 22.8 us -> 21 us  [the longest x1 21 us: local(): lax.all_to_all(both_rows, 'enc', split_axis=0, concat_axis=0, tiled=True)]
    reduce_sum x2 -> x0, other arithmetic: 1.77 us -> none  [attend_all(): jnp.sum(grad_scores, axis=0).reshape(BLOCK_LEN, pool_size, PASSAGE)]
    another operation x2 -> x0, other arithmetic: 1.43 us -> none  [the longest x1 1.33 us: local(): jnp.stack([queries.reshape(blocks_here, BLOCK_LEN, full_width), cotangent...]
  transfers between devices with their start and end apart: 2 -> 2, of which waited for: 1 -> 1; matrix products, arithmetic and copies ran while one was open for 9% -> 3% of each run, Pallas kernels for 0% -> 0%
where the time goes in v2:
time: 111 us
  blocking collectives  38.5 us (35%)
  starting transfers between devices  23.3 us (21%)
  waiting for transfers between devices  21 us (19%)
  Pallas kernels  15.4 us (14%)
  local copies, waits for them, and re-layouts  10.8 us (10%)
  other arithmetic  1.14 us (1%)
    psum x2, blocking collectives, reduce_groups(): return lax.psum(lax.psum(part, 'dp'), 'seq')  38.5 us
    all_to_all x1, waiting for transfers between devices, local(): lax.all_to_all(both_rows, 'enc', split_axis=0, concat_axis=0, tiled=True)  21 us
    all_to_all x1, starting transfers between devices, local(): lax.all_to_all(both_rows, 'enc', split_axis=0, concat_axis=0, tiled=True)  16.6 us
    pallas_call x1, Pallas kernels, attend_all(): pl.pallas_call(attend_kernel, grid=grid, in_specs=[pl.BlockSpec((seqs_ste...  15.4 us
    unnamed x19, local copies, waits for them, and re-layouts  7.48 us
    all_to_all x1, starting transfers between devices, local(): lax.all_to_all(both_out, 'enc', split_axis=0, concat_axis=0, tiled=True)  6.74 us
  transfers between devices with their start and end apart: 2, of which 1 were waited for; matrix products, arithmetic and copies ran while one was open for 3% of the time, Pallas kernels for 0%

profile of v2, /device:TPU:16, one launch (start us, length us, event | category | flops | bytes accessed | tf_op | source)
XLA Modules:
  0.0 110.9 jit_solution(17333861219679479938)
XLA Ops:
  0.6 1.3 %copy.24 = bf16[1,128,2048]{1,2,0:T(8,128)(2,1)S(1)} copy(bf16[1,128,2048]{2,1,0:T(8,128)(2,1)} %param.7) | data formatting | bytes 1048576 | tf_op args[0]
  2.0 0.3 copy.26
  2.2 0.8 copy-done.1
  3.0 0.3 copy.25
  3.3 0.3 copy.27
  3.6 1.1 maximum_bitcast_fusion
  4.7 16.6 %all-to-all-start = ((bf16[16,2,128,128]{3,2,1,0:T(8,128)(2,1)}), bf16[16,2,128,128]{3,2,1,0:T(8,128)(2,1)S(1)}, u32[]{:S(2)}, u32[]{:S(2)}) async-start(bf16[16,2,128,128]{3,2,1,0:T(8,128)(2,1)} %maximum_bitcast_fusion), calls=%async_computation | async-start | bytes 2097152 | tf_op jit(solution)/shard_map/all_to_all | solution.py:159
  21.2 0.1 copy.28
  21.3 0.1 lt.20
  21.4 0.6 copy-done.3
  22.0 0.1 copy.29
  22.1 0.1 copy.30
  22.3 0.6 copy-done.5
  22.9 0.1 broadcast_in_dim.21
  23.0 0.1 slice_reduce_fusion
  23.1 0.2 reshape.67
  23.3 0.1 broadcast_in_dim.22
  23.4 0.7 reshape_reshape.11.mask_ref
  24.3 0.8 copy.38
  25.0 21.0 %all-to-all-done.qd_ref = bf16[16,2,128,128]{3,2,1,0:T(8,128)(2,1)S(1)} async-done(((bf16[16,2,128,128]{3,2,1,0:T(8,128)(2,1)}), bf16[16,2,128,128]{3,2,1,0:T(8,128)(2,1)S(1)}, u32[]{:S(2)}, u32[]{:S(2)}) %all-to-all-start) | async-done | bytes 1048608 | tf_op jit(solution)/shard_map/all_to_all | solution.py:159
  46.0 1.0 copy-done
  47.0 15.4 %shard_map.110 = (bf16[16,2,128,128]{3,2,1,0:T(8,128)(2,1)}, bf16[1024,128]{1,0:T(8,128)(2,1)}, bf16[1024,128]{1,0:T(8,128)(2,1)}, f32[64,128]{1,0:T(8,128)}) custom-call(bf16[16,2,128,128]{3,2,1,0:T(8,128)(2,1)} %copy-done, bf16[1024,128]{1,0:T(8,128)(2,1)} %bitcast.29, bf16[1024,128]{1,0:T(8,128)(2,1)} %bitcast.30, f32[64,1024]{1,0:T(8,128)} %bitcast.27, ...), custom_call_target="tpu_custom_call" | custom-call | tf_op jit(solution)/shard_map/pallas_call | solution.py:106
  62.3 6.7 %all-to-all-start.1 = ((bf16[16,2,128,128]{3,2,1,0:T(8,128)(2,1)}), bf16[16,2,128,128]{3,2,1,0:T(8,128)(2,1)S(1)}, u32[]{:S(2)}, u32[]{:S(2)}) async-start(bf16[16,2,128,128]{3,2,1,0:T(8,128)(2,1)} %get-tuple-element.9), calls=%async_computation.1 | async-start | bytes 2097152 | tf_op jit(solution)/shard_map/all_to_all | solution.py:163
  69.2 0.3 reshape.70
  69.4 0.1 pad_reduce_fusion
  69.7 14.2 %psum.14 = f32[1,191]{1,0:T(1,128)S(1)} all-reduce(f32[1,191]{1,0:T(1,128)S(1)} %bitcast.33), channel_id=1, replica_groups=mesh['dp'=8,'seq'=8,'enc'=16] {'dp'}, use_global_device_ids=true, to_apply=%region_2.3 | all-reduce | flops 191 | bytes 1528 | tf_op jit(solution)/shard_map/psum | solution.py:138
  83.8 24.4 %psum.15 = f32[1,191]{1,0:T(1,128)} all-reduce(f32[1,191]{1,0:T(1,128)S(1)} %psum.14), channel_id=1, replica_groups=mesh['dp'=8,'seq'=8,'enc'=16] {'seq'}, use_global_device_ids=true, to_apply=%region_3.4 | all-reduce | flops 191 | bytes 1528 | tf_op jit(solution)/shard_map/psum | solution.py:138
  108.2 0.1 fusion.2
  108.3 0.3 copy.33
  108.6 1.0 copy.35
  109.6 0.3 copy.32
  109.9 1.0 copy.34
  (20 shorter events, 0.4 us)
Async XLA Ops:
  1.9 1.0 copy-start.1
  4.6 16.6 %copy-start.4 = (s32[16,2]{0,1:T(2,128)S(1)}, s32[16,2]{0,1:T(2,128)}, u32[]{:S(2)}) copy-start(s32[16,2]{0,1:T(2,128)} %param.11) | copy-start | bytes 388
  4.7 41.3 %all-to-all-start = ((bf16[16,2,128,128]{3,2,1,0:T(8,128)(2,1)}), bf16[16,2,128,128]{3,2,1,0:T(8,128)(2,1)S(1)}, u32[]{:S(2)}, u32[]{:S(2)}) async-start(bf16[16,2,128,128]{3,2,1,0:T(8,128)(2,1)} %maximum_bitcast_fusion), calls=%async_computation | async-start | bytes 2097152 | tf_op jit(solution)/shard_map/all_to_all | solution.py:159
  21.3 0.7 copy-start.3
  22.2 0.7 copy-start.5
  46.0 1.0 copy-start
  62.3 6.8 %copy-start.2 = (f32[64,128]{1,0:T(8,128)S(1)}, f32[64,128]{1,0:T(8,128)}, u32[]{:S(2)}) copy-start(f32[64,128]{1,0:T(8,128)} %get-tuple-element.12) | copy-start | bytes 98308
  62.3 45.9 %all-to-all-start.1 = ((bf16[16,2,128,128]{3,2,1,0:T(8,128)(2,1)}), bf16[16,2,128,128]{3,2,1,0:T(8,128)(2,1)S(1)}, u32[]{:S(2)}, u32[]{:S(2)}) async-start(bf16[16,2,128,128]{3,2,1,0:T(8,128)(2,1)} %get-tuple-element.9), calls=%async_computation.1 | async-start | bytes 2097152 | tf_op jit(solution)/shard_map/all_to_all | solution.py:163

commit v3 on v2

--- a/solution.py
+++ b/solution.py
@@ -1,3 +1,4 @@
+import functools
 import math
 
 import jax
@@ -134,11 +135,18 @@
     )(both_heads, keys_flat, values_flat, bias_wide, usable)
 
 
-def reduce_groups(part):
-    return lax.psum(lax.psum(part, "dp"), "seq")
-
-
-def local(queries, cotangent, key_pool, value_pool, counts, neighbour_ids, rel_bias):
+def reduce_groups(part, mesh_shape):
+    for axis in ("dp", "seq"):
+        size = mesh_shape[axis]
+        step = 1
+        while step < size:
+            pairs = [(index, index ^ step) for index in range(size)]
+            part = part + lax.ppermute(part, axis, pairs)
+            step *= 2
+    return part
+
+
+def local(mesh_shape, queries, cotangent, key_pool, value_pool, counts, neighbour_ids, rel_bias):
     token_rows = queries.shape[1]
     full_width = queries.shape[2]
     blocks_here = token_rows // BLOCK_LEN
@@ -162,7 +170,7 @@
     )
     both_back = lax.all_to_all(both_out, "enc", split_axis=0, concat_axis=0, tiled=True)
     both_back = both_back.transpose(1, 2, 0, 3).reshape((2,) + queries.shape)
-    bias_grad = reduce_groups(fold_bias(bias_total[None], rel_bias.shape[1]))
+    bias_grad = reduce_groups(fold_bias(bias_total[None], rel_bias.shape[1]), mesh_shape)
     return (
         both_back[0],
         both_back[1],
@@ -189,4 +197,4 @@
         P("dp", "seq", None, None, "enc"),
         P("enc", None),
     )
-    return jax.shard_map(local, mesh=mesh, in_specs=in_specs, out_specs=out_specs, check_vma=False)
+    return jax.shard_map(functools.partial(local, dict(mesh.shape)), mesh=mesh, in_specs=in_specs, out_specs=out_specs, check_vma=False)

time: 111 us -> 116 us (1.045)
  blocking collectives: 38.5 us -> 0 us
  waiting for transfers between devices: 21 us -> 46.1 us
  starting transfers between devices: 23.3 us -> 40.5 us
    psum x2 -> x0, blocking collectives: 38.5 us -> none  [reduce_groups(): return lax.psum(lax.psum(part, 'dp'), 'seq')]
    ppermute x0 -> x6, waiting for transfers between devices: none -> 25.1 us  [reduce_groups(): part = part + lax.ppermute(part, axis, pairs)]
    ppermute x0 -> x6, starting transfers between devices: none -> 17.2 us  [reduce_groups(): part = part + lax.ppermute(part, axis, pairs)]
  transfers between devices with their start and end apart: 2 -> 8, of which waited for: 1 -> 7; matrix products, arithmetic and copies ran while one was open for 3% -> 3% of each run, Pallas kernels for 0% -> 0%
where the time goes in v3:
time: 116 us; the launch traced here: 115 us
  waiting for transfers between devices  46.1 us (40%)
  starting transfers between devices  40.5 us (35%)
  Pallas kernels  15.3 us (13%)
  local copies, waits for them, and re-layouts  10.8 us (9%)
  other arithmetic  1.7 us (1%)
    ppermute x6, waiting for transfers between devices, reduce_groups(): part = part + lax.ppermute(part, axis, pairs)  25.1 us
    all_to_all x1, waiting for transfers between devices, local(): lax.all_to_all(both_rows, 'enc', split_axis=0, concat_axis=0, tiled=True)  21 us
    ppermute x6, starting transfers between devices, reduce_groups(): part = part + lax.ppermute(part, axis, pairs)  17.2 us
    all_to_all x1, starting transfers between devices, local(): lax.all_to_all(both_rows, 'enc', split_axis=0, concat_axis=0, tiled=True)  16.6 us
    pallas_call x1, Pallas kernels, attend_all(): pl.pallas_call(attend_kernel, grid=grid, in_specs=[pl.BlockSpec((seqs_ste...  15.3 us
    unnamed x19, local copies, waits for them, and re-layouts  7.46 us
    all_to_all x1, starting transfers between devices, local(): lax.all_to_all(both_out, 'enc', split_axis=0, concat_axis=0, tiled=True)  6.75 us
  transfers between devices with their start and end apart: 8, of which 7 were waited for; matrix products, arithmetic and copies ran while one was open for 3% of the time, Pallas kernels for 0%

profile of v3, /device:TPU:16, one launch (start us, length us, event | category | flops | bytes accessed | tf_op | source)
XLA Modules:
  0.0 115.2 jit_solution(14187271825203411198)
XLA Ops:
  0.6 1.3 %copy.24 = bf16[1,128,2048]{1,2,0:T(8,128)(2,1)S(1)} copy(bf16[1,128,2048]{2,1,0:T(8,128)(2,1)} %param.7) | data formatting | bytes 1048576 | tf_op args[0]
  2.0 0.3 copy.26
  2.2 0.8 copy-done.1
  3.0 0.3 copy.25
  3.3 0.3 copy.27
  3.6 1.1 maximum_bitcast_fusion
  4.6 16.6 %all-to-all-start = ((bf16[16,2,128,128]{3,2,1,0:T(8,128)(2,1)}), bf16[16,2,128,128]{3,2,1,0:T(8,128)(2,1)S(1)}, u32[]{:S(2)}, u32[]{:S(2)}) async-start(bf16[16,2,128,128]{3,2,1,0:T(8,128)(2,1)} %maximum_bitcast_fusion), calls=%async_computation | async-start | bytes 2097152 | tf_op jit(solution)/shard_map/all_to_all | solution.py:167
  21.4 0.6 copy-done.3
  22.3 0.6 copy-done.5
  23.4 0.7 reshape_reshape.11.mask_ref
  24.3 0.8 copy.38
  25.0 21.0 %all-to-all-done.qd_ref = bf16[16,2,128,128]{3,2,1,0:T(8,128)(2,1)S(1)} async-done(((bf16[16,2,128,128]{3,2,1,0:T(8,128)(2,1)}), bf16[16,2,128,128]{3,2,1,0:T(8,128)(2,1)S(1)}, u32[]{:S(2)}, u32[]{:S(2)}) %all-to-all-start) | async-done | bytes 1048608 | tf_op jit(solution)/shard_map/all_to_all | solution.py:167
  46.0 1.0 copy-done
  46.9 15.3 %shard_map.110 = (bf16[16,2,128,128]{3,2,1,0:T(8,128)(2,1)}, bf16[1024,128]{1,0:T(8,128)(2,1)}, bf16[1024,128]{1,0:T(8,128)(2,1)}, f32[64,128]{1,0:T(8,128)}) custom-call(bf16[16,2,128,128]{3,2,1,0:T(8,128)(2,1)} %copy-done, bf16[1024,128]{1,0:T(8,128)(2,1)} %bitcast.29, bf16[1024,128]{1,0:T(8,128)(2,1)} %bitcast.30, f32[64,1024]{1,0:T(8,128)} %bitcast.27, ...), custom_call_target="tpu_custom_call" | custom-call | tf_op jit(solution)/shard_map/pallas_call | solution.py:107
  62.3 6.8 %all-to-all-start.1 = ((bf16[16,2,128,128]{3,2,1,0:T(8,128)(2,1)}), bf16[16,2,128,128]{3,2,1,0:T(8,128)(2,1)S(1)}, u32[]{:S(2)}, u32[]{:S(2)}) async-start(bf16[16,2,128,128]{3,2,1,0:T(8,128)(2,1)} %get-tuple-element.9), calls=%async_computation.1 | async-start | bytes 2097152 | tf_op jit(solution)/shard_map/all_to_all | solution.py:171
  69.6 1.9 %collective-permute-start = (f32[1,191]{1,0:T(1,128)S(1)}, f32[1,191]{1,0:T(1,128)S(1)}, u32[]{:S(2)}, u32[]{:S(2)}) collective-permute-start(f32[1,191]{1,0:T(1,128)S(1)} %bitcast.33), channel_id=1, source_target_pairs={{0,128},{128,0},{256,384},{384,256},{512,640},{640,512},{768,896},... | collective-permute-start | bytes 2300 | tf_op jit(solution)/shard_map/ppermute | solution.py:144
  71.5 3.5 %collective-permute-done = f32[1,191]{1,0:T(1,128)S(1)} collective-permute-done((f32[1,191]{1,0:T(1,128)S(1)}, f32[1,191]{1,0:T(1,128)S(1)}, u32[]{:S(2)}, u32[]{:S(2)}) %collective-permute-start) | collective-permute-done | bytes 796 | tf_op jit(solution)/shard_map/ppermute | solution.py:144
  75.1 1.9 %collective-permute-start.1 = (f32[1,191]{1,0:T(1,128)S(1)}, f32[1,191]{1,0:T(1,128)S(1)}, u32[]{:S(2)}, u32[]{:S(2)}) collective-permute-start(f32[1,191]{1,0:T(1,128)S(1)} %slice_add_fusion), channel_id=1, source_target_pairs={{0,256},{128,384},{256,0},{384,128},{512,768},{640,896},{768,512},... | collective-permute-start | bytes 2300 | tf_op jit(solution)/shard_map/ppermute | solution.py:144
  77.0 4.4 %collective-permute-done.1 = f32[1,191]{1,0:T(1,128)S(1)} collective-permute-done((f32[1,191]{1,0:T(1,128)S(1)}, f32[1,191]{1,0:T(1,128)S(1)}, u32[]{:S(2)}, u32[]{:S(2)}) %collective-permute-start.1) | collective-permute-done | bytes 796 | tf_op jit(solution)/shard_map/ppermute | solution.py:144
  81.4 1.9 %collective-permute-start.2 = (f32[1,191]{1,0:T(1,128)S(1)}, f32[1,191]{1,0:T(1,128)S(1)}, u32[]{:S(2)}, u32[]{:S(2)}) collective-permute-start(f32[1,191]{1,0:T(1,128)S(1)} %add.25), channel_id=1, source_target_pairs={{0,512},{128,640},{256,768},{384,896},{512,0},{640,128},{768,256},... | collective-permute-start | bytes 2300 | tf_op jit(solution)/shard_map/ppermute | solution.py:144
  83.4 7.4 %collective-permute-done.2 = f32[1,191]{1,0:T(1,128)S(1)} collective-permute-done((f32[1,191]{1,0:T(1,128)S(1)}, f32[1,191]{1,0:T(1,128)S(1)}, u32[]{:S(2)}, u32[]{:S(2)}) %collective-permute-start.2) | collective-permute-done | bytes 796 | tf_op jit(solution)/shard_map/ppermute | solution.py:144
  90.8 1.9 %collective-permute-start.3 = (f32[1,191]{1,0:T(1,128)S(1)}, f32[1,191]{1,0:T(1,128)S(1)}, u32[]{:S(2)}, u32[]{:S(2)}) collective-permute-start(f32[1,191]{1,0:T(1,128)S(1)} %add.26), channel_id=1, source_target_pairs={{0,16},{16,0},{32,48},{48,32},{64,80},{80,64},{96,112},{112,96},{1... | collective-permute-start | bytes 2300 | tf_op jit(solution)/shard_map/ppermute | solution.py:144
  92.7 3.5 %collective-permute-done.3 = f32[1,191]{1,0:T(1,128)S(1)} collective-permute-done((f32[1,191]{1,0:T(1,128)S(1)}, f32[1,191]{1,0:T(1,128)S(1)}, u32[]{:S(2)}, u32[]{:S(2)}) %collective-permute-start.3) | collective-permute-done | bytes 796 | tf_op jit(solution)/shard_map/ppermute | solution.py:144
  96.3 1.9 %collective-permute-start.4 = (f32[1,191]{1,0:T(1,128)S(1)}, f32[1,191]{1,0:T(1,128)S(1)}, u32[]{:S(2)}, u32[]{:S(2)}) collective-permute-start(f32[1,191]{1,0:T(1,128)S(1)} %add.27), channel_id=1, source_target_pairs={{0,32},{16,48},{32,0},{48,16},{64,96},{80,112},{96,64},{112,80},{1... | collective-permute-start | bytes 2300 | tf_op jit(solution)/shard_map/ppermute | solution.py:144
  98.2 4.4 %collective-permute-done.4 = f32[1,191]{1,0:T(1,128)S(1)} collective-permute-done((f32[1,191]{1,0:T(1,128)S(1)}, f32[1,191]{1,0:T(1,128)S(1)}, u32[]{:S(2)}, u32[]{:S(2)}) %collective-permute-start.4) | collective-permute-done | bytes 796 | tf_op jit(solution)/shard_map/ppermute | solution.py:144
  102.6 7.6 %collective-permute-start.5 = (f32[1,191]{1,0:T(1,128)S(1)}, f32[1,191]{1,0:T(1,128)S(1)}, u32[]{:S(2)}, u32[]{:S(2)}) collective-permute-start(f32[1,191]{1,0:T(1,128)S(1)} %add.28), channel_id=1, source_target_pairs={{0,64},{16,80},{32,96},{48,112},{64,0},{80,16},{96,32},{112,48},{1... | collective-permute-start | bytes 2300 | tf_op jit(solution)/shard_map/ppermute | solution.py:144
  110.3 1.7 %collective-permute-done.5 = f32[1,191]{1,0:T(1,128)S(1)} collective-permute-done((f32[1,191]{1,0:T(1,128)S(1)}, f32[1,191]{1,0:T(1,128)S(1)}, u32[]{:S(2)}, u32[]{:S(2)}) %collective-permute-start.5) | collective-permute-done | bytes 796 | tf_op jit(solution)/shard_map/ppermute | solution.py:144
  112.0 0.6 add.29
  112.6 0.3 copy.33
  112.9 1.0 copy.35
  114.0 0.3 copy.32
  114.2 1.0 copy.34
  (36 shorter events, 1.8 us)
Async XLA Ops:
  1.9 1.0 copy-start.1
  4.6 16.6 %copy-start.4 = (s32[16,2]{0,1:T(2,128)S(1)}, s32[16,2]{0,1:T(2,128)}, u32[]{:S(2)}) copy-start(s32[16,2]{0,1:T(2,128)} %param.11) | copy-start | bytes 388
  4.6 41.3 %all-to-all-start = ((bf16[16,2,128,128]{3,2,1,0:T(8,128)(2,1)}), bf16[16,2,128,128]{3,2,1,0:T(8,128)(2,1)S(1)}, u32[]{:S(2)}, u32[]{:S(2)}) async-start(bf16[16,2,128,128]{3,2,1,0:T(8,128)(2,1)} %maximum_bitcast_fusion), calls=%async_computation | async-start | bytes 2097152 | tf_op jit(solution)/shard_map/all_to_all | solution.py:167
  21.3 0.7 copy-start.3
  22.2 0.7 copy-start.5
  46.0 1.0 copy-start
  62.3 6.8 %copy-start.2 = (f32[64,128]{1,0:T(8,128)S(1)}, f32[64,128]{1,0:T(8,128)}, u32[]{:S(2)}) copy-start(f32[64,128]{1,0:T(8,128)} %get-tuple-element.12) | copy-start | bytes 98308
  62.3 50.2 %all-to-all-start.1 = ((bf16[16,2,128,128]{3,2,1,0:T(8,128)(2,1)}), bf16[16,2,128,128]{3,2,1,0:T(8,128)(2,1)S(1)}, u32[]{:S(2)}, u32[]{:S(2)}) async-start(bf16[16,2,128,128]{3,2,1,0:T(8,128)(2,1)} %get-tuple-element.9), calls=%async_computation.1 | async-start | bytes 2097152 | tf_op jit(solution)/shard_map/all_to_all | solution.py:171
  69.6 5.5 %collective-permute-start = (f32[1,191]{1,0:T(1,128)S(1)}, f32[1,191]{1,0:T(1,128)S(1)}, u32[]{:S(2)}, u32[]{:S(2)}) collective-permute-start(f32[1,191]{1,0:T(1,128)S(1)} %bitcast.33), channel_id=1, source_target_pairs={{0,128},{128,0},{256,384},{384,256},{512,640},{640,512},{768,896},... | collective-permute-start | bytes 2300 | tf_op jit(solution)/shard_map/ppermute | solution.py:144
  75.1 6.3 %collective-permute-start.1 = (f32[1,191]{1,0:T(1,128)S(1)}, f32[1,191]{1,0:T(1,128)S(1)}, u32[]{:S(2)}, u32[]{:S(2)}) collective-permute-start(f32[1,191]{1,0:T(1,128)S(1)} %slice_add_fusion), channel_id=1, source_target_pairs={{0,256},{128,384},{256,0},{384,128},{512,768},{640,896},{768,512},... | collective-permute-start | bytes 2300 | tf_op jit(solution)/shard_map/ppermute | solution.py:144
  81.4 9.4 %collective-permute-start.2 = (f32[1,191]{1,0:T(1,128)S(1)}, f32[1,191]{1,0:T(1,128)S(1)}, u32[]{:S(2)}, u32[]{:S(2)}) collective-permute-start(f32[1,191]{1,0:T(1,128)S(1)} %add.25), channel_id=1, source_target_pairs={{0,512},{128,640},{256,768},{384,896},{512,0},{640,128},{768,256},... | collective-permute-start | bytes 2300 | tf_op jit(solution)/shard_map/ppermute | solution.py:144
  90.8 5.5 %collective-permute-start.3 = (f32[1,191]{1,0:T(1,128)S(1)}, f32[1,191]{1,0:T(1,128)S(1)}, u32[]{:S(2)}, u32[]{:S(2)}) collective-permute-start(f32[1,191]{1,0:T(1,128)S(1)} %add.26), channel_id=1, source_target_pairs={{0,16},{16,0},{32,48},{48,32},{64,80},{80,64},{96,112},{112,96},{1... | collective-permute-start | bytes 2300 | tf_op jit(solution)/shard_map/ppermute | solution.py:144
  96.3 6.3 %collective-permute-start.4 = (f32[1,191]{1,0:T(1,128)S(1)}, f32[1,191]{1,0:T(1,128)S(1)}, u32[]{:S(2)}, u32[]{:S(2)}) collective-permute-start(f32[1,191]{1,0:T(1,128)S(1)} %add.27), channel_id=1, source_target_pairs={{0,32},{16,48},{32,0},{48,16},{64,96},{80,112},{96,64},{112,80},{1... | collective-permute-start | bytes 2300 | tf_op jit(solution)/shard_map/ppermute | solution.py:144
  102.6 9.4 %collective-permute-start.5 = (f32[1,191]{1,0:T(1,128)S(1)}, f32[1,191]{1,0:T(1,128)S(1)}, u32[]{:S(2)}, u32[]{:S(2)}) collective-permute-start(f32[1,191]{1,0:T(1,128)S(1)} %add.28), channel_id=1, source_target_pairs={{0,64},{16,80},{32,96},{48,112},{64,0},{80,16},{96,32},{112,48},{1... | collective-permute-start | bytes 2300 | tf_op jit(solution)/shard_map/ppermute | solution.py:144

commit v4 on v2

--- a/solution.py
+++ b/solution.py
@@ -59,10 +59,13 @@
     scores = lax.dot_general(query_rows, keys, contract_last, preferred_element_type=jnp.float32)
     scores = scores.reshape(tile4) * score_scale + bias_ref[...][None, None]
     usable = mask_ref[...][:, :, None, :] > 0.5
-    row_top = jnp.max(jnp.where(usable, scores, NEG_FILL), axis=3, keepdims=True)
-    raised = jnp.where(usable, jnp.exp(scores - row_top), 0.0)
+    masked = jnp.where(usable, scores, NEG_FILL)
+    row_top = jnp.max(masked, axis=3, keepdims=True)
+    raised = jnp.exp(masked - row_top)
     total = jnp.sum(raised, axis=3, keepdims=True)
-    weights = raised / (total + jnp.where(total == 0.0, 1.0, 0.0))
+    any_used = jnp.max(mask_ref[...], axis=2, keepdims=True)[:, :, :, None] > 0.5
+    row_scale = jnp.where(any_used, 1.0 / total, 0.0)
+    weights = raised * row_scale
     weights_low = weights.astype(jnp.bfloat16).reshape(rows, width)
     context = jnp.dot(weights_low, values, preferred_element_type=jnp.float32)
     grad_weights = lax.dot_general(grad_rows, values, contract_last, preferred_element_type=jnp.float32)

time: 111 us -> 111 us (level)
  no operation moved by 1% of the time
where the time goes in v4:
time: 111 us; the launch traced here: 110 us
  blocking collectives  38.5 us (35%)
  starting transfers between devices  23.3 us (21%)
  waiting for transfers between devices  21 us (19%)
  Pallas kernels  14.9 us (13%)
  local copies, waits for them, and re-layouts  10.8 us (10%)
  other arithmetic  1.14 us (1%)
    psum x2, blocking collectives, reduce_groups(): return lax.psum(lax.psum(part, 'dp'), 'seq')  38.5 us
    all_to_all x1, waiting for transfers between devices, local(): lax.all_to_all(both_rows, 'enc', split_axis=0, concat_axis=0, tiled=True)  21 us
    all_to_all x1, starting transfers between devices, local(): lax.all_to_all(both_rows, 'enc', split_axis=0, concat_axis=0, tiled=True)  16.6 us
    pallas_call x1, Pallas kernels, attend_all(): pl.pallas_call(attend_kernel, grid=grid, in_specs=[pl.BlockSpec((seqs_ste...  14.9 us
    unnamed x19, local copies, waits for them, and re-layouts  7.48 us
    all_to_all x1, starting transfers between devices, local(): lax.all_to_all(both_out, 'enc', split_axis=0, concat_axis=0, tiled=True)  6.74 us
  transfers between devices with their start and end apart: 2, of which 1 were waited for; matrix products, arithmetic and copies ran while one was open for 3% of the time, Pallas kernels for 0%

profile of v4, /device:TPU:16, one launch (start us, length us, event | category | flops | bytes accessed | tf_op | source)
XLA Modules:
  0.0 110.5 jit_solution(86257336105661479)
XLA Ops:
  0.6 1.3 %copy.24 = bf16[1,128,2048]{1,2,0:T(8,128)(2,1)S(1)} copy(bf16[1,128,2048]{2,1,0:T(8,128)(2,1)} %param.7) | data formatting | bytes 1048576 | tf_op args[0]
  2.0 0.3 copy.26
  2.2 0.8 copy-done.1
  3.0 0.3 copy.25
  3.3 0.3 copy.27
  3.6 1.1 maximum_bitcast_fusion
  4.7 16.6 %all-to-all-start = ((bf16[16,2,128,128]{3,2,1,0:T(8,128)(2,1)}), bf16[16,2,128,128]{3,2,1,0:T(8,128)(2,1)S(1)}, u32[]{:S(2)}, u32[]{:S(2)}) async-start(bf16[16,2,128,128]{3,2,1,0:T(8,128)(2,1)} %maximum_bitcast_fusion), calls=%async_computation | async-start | bytes 2097152 | tf_op jit(solution)/shard_map/all_to_all | solution.py:162
  21.2 0.1 copy.28
  21.3 0.1 lt.20
  21.4 0.6 copy-done.3
  22.0 0.1 copy.29
  22.1 0.1 copy.30
  22.3 0.6 copy-done.5
  22.9 0.1 broadcast_in_dim.21
  23.0 0.1 slice_reduce_fusion
  23.1 0.2 reshape.67
  23.3 0.1 broadcast_in_dim.22
  23.4 0.7 reshape_reshape.11.mask_ref
  24.3 0.8 copy.38
  25.0 21.0 %all-to-all-done.qd_ref = bf16[16,2,128,128]{3,2,1,0:T(8,128)(2,1)S(1)} async-done(((bf16[16,2,128,128]{3,2,1,0:T(8,128)(2,1)}), bf16[16,2,128,128]{3,2,1,0:T(8,128)(2,1)S(1)}, u32[]{:S(2)}, u32[]{:S(2)}) %all-to-all-start) | async-done | bytes 1048608 | tf_op jit(solution)/shard_map/all_to_all | solution.py:162
  46.0 1.0 copy-done
  47.0 14.9 %shard_map.110 = (bf16[16,2,128,128]{3,2,1,0:T(8,128)(2,1)}, bf16[1024,128]{1,0:T(8,128)(2,1)}, bf16[1024,128]{1,0:T(8,128)(2,1)}, f32[64,128]{1,0:T(8,128)}) custom-call(bf16[16,2,128,128]{3,2,1,0:T(8,128)(2,1)} %copy-done, bf16[1024,128]{1,0:T(8,128)(2,1)} %bitcast.29, bf16[1024,128]{1,0:T(8,128)(2,1)} %bitcast.30, f32[64,1024]{1,0:T(8,128)} %bitcast.27, ...), custom_call_target="tpu_custom_call" | custom-call | tf_op jit(solution)/shard_map/pallas_call | solution.py:109
  61.9 6.7 %all-to-all-start.1 = ((bf16[16,2,128,128]{3,2,1,0:T(8,128)(2,1)}), bf16[16,2,128,128]{3,2,1,0:T(8,128)(2,1)S(1)}, u32[]{:S(2)}, u32[]{:S(2)}) async-start(bf16[16,2,128,128]{3,2,1,0:T(8,128)(2,1)} %get-tuple-element.9), calls=%async_computation.1 | async-start | bytes 2097152 | tf_op jit(solution)/shard_map/all_to_all | solution.py:166
  68.7 0.3 reshape.70
  69.0 0.1 pad_reduce_fusion
  69.2 14.2 %psum.14 = f32[1,191]{1,0:T(1,128)S(1)} all-reduce(f32[1,191]{1,0:T(1,128)S(1)} %bitcast.33), channel_id=1, replica_groups=mesh['dp'=8,'seq'=8,'enc'=16] {'dp'}, use_global_device_ids=true, to_apply=%region_2.3 | all-reduce | flops 191 | bytes 1528 | tf_op jit(solution)/shard_map/psum | solution.py:141
  83.4 24.4 %psum.15 = f32[1,191]{1,0:T(1,128)} all-reduce(f32[1,191]{1,0:T(1,128)S(1)} %psum.14), channel_id=1, replica_groups=mesh['dp'=8,'seq'=8,'enc'=16] {'seq'}, use_global_device_ids=true, to_apply=%region_3.4 | all-reduce | flops 191 | bytes 1528 | tf_op jit(solution)/shard_map/psum | solution.py:141
  107.8 0.1 fusion.2
  107.9 0.3 copy.33
  108.2 1.0 copy.35
  109.2 0.3 copy.32
  109.5 1.0 copy.34
  (20 shorter events, 0.4 us)
Async XLA Ops:
  1.9 1.0 copy-start.1
  4.6 16.6 %copy-start.4 = (s32[16,2]{0,1:T(2,128)S(1)}, s32[16,2]{0,1:T(2,128)}, u32[]{:S(2)}) copy-start(s32[16,2]{0,1:T(2,128)} %param.11) | copy-start | bytes 388
  4.7 41.3 %all-to-all-start = ((bf16[16,2,128,128]{3,2,1,0:T(8,128)(2,1)}), bf16[16,2,128,128]{3,2,1,0:T(8,128)(2,1)S(1)}, u32[]{:S(2)}, u32[]{:S(2)}) async-start(bf16[16,2,128,128]{3,2,1,0:T(8,128)(2,1)} %maximum_bitcast_fusion), calls=%async_computation | async-start | bytes 2097152 | tf_op jit(solution)/shard_map/all_to_all | solution.py:162
  21.3 0.7 copy-start.3
  22.2 0.7 copy-start.5
  46.0 1.0 copy-start
  61.9 6.8 %copy-start.2 = (f32[64,128]{1,0:T(8,128)S(1)}, f32[64,128]{1,0:T(8,128)}, u32[]{:S(2)}) copy-start(f32[64,128]{1,0:T(8,128)} %get-tuple-element.12) | copy-start | bytes 98308
  61.9 45.9 %all-to-all-start.1 = ((bf16[16,2,128,128]{3,2,1,0:T(8,128)(2,1)}), bf16[16,2,128,128]{3,2,1,0:T(8,128)(2,1)S(1)}, u32[]{:S(2)}, u32[]{:S(2)}) async-start(bf16[16,2,128,128]{3,2,1,0:T(8,128)(2,1)} %get-tuple-element.9), calls=%async_computation.1 | async-start | bytes 2097152 | tf_op jit(solution)/shard_map/all_to_all | solution.py:166

commit v5 on v4

--- a/solution.py
+++ b/solution.py
@@ -82,28 +82,18 @@
 
     @pl.when(step == pl.num_programs(0) - 1)
     def _():
-        key_out[...] = (score_scale * key_acc[...]).astype(key_out.dtype)
-        value_out[...] = value_acc[...].astype(value_out.dtype)
+        key_out[...] = key_acc[...]
+        value_out[...] = value_acc[...]
         folded = bias_acc[:, 0:PASSAGE]
         for part in range(1, width // PASSAGE):
             folded = folded + bias_acc[:, part * PASSAGE:(part + 1) * PASSAGE]
         bias_out[...] = folded
 
 
-def attend_all(both_heads, id_table, count_table, pool_keys, pool_values, row_bias):
+def attend_all(both_heads, usable, keys_flat, values_flat, bias_wide):
     seq_total, halves, rows_seq, _ = both_heads.shape
-    pool_size = pool_keys.shape[0]
-    width = pool_size * PASSAGE
+    width = keys_flat.shape[0]
     blocks_seq = rows_seq // BLOCK_LEN
-    keys_flat = pool_keys.reshape(width, HEAD_DIM)
-    values_flat = pool_values.reshape(width, HEAD_DIM)
-    slot_index = jnp.arange(id_table.shape[1])
-    picked = (slot_index[None, :] < count_table[:, None])[:, :, None] & (
-        id_table[:, :, None] == jnp.arange(pool_size)[None, None, :]
-    )
-    usable = jnp.repeat(jnp.any(picked, axis=1).astype(jnp.float32), PASSAGE, axis=1)
-    usable = usable.reshape(seq_total, blocks_seq, width)
-    bias_wide = jnp.tile(row_bias[0], (1, pool_size))
     seqs_step = 2
     grid = (seq_total // seqs_step,)
     return pl.pallas_call(
@@ -124,8 +114,8 @@
         ],
         out_shape=[
             jax.ShapeDtypeStruct(both_heads.shape, jnp.bfloat16),
-            jax.ShapeDtypeStruct((width, HEAD_DIM), jnp.bfloat16),
-            jax.ShapeDtypeStruct((width, HEAD_DIM), jnp.bfloat16),
+            jax.ShapeDtypeStruct((width, HEAD_DIM), jnp.float32),
+            jax.ShapeDtypeStruct((width, HEAD_DIM), jnp.float32),
             jax.ShapeDtypeStruct((BLOCK_LEN, PASSAGE), jnp.float32),
         ],
         scratch_shapes=[
@@ -153,17 +143,38 @@
     id_table = neighbour_ids.reshape(-1, neighbour_ids.shape[-1])
     count_table = counts.reshape(-1)
     row_bias = bias_rows(rel_bias)
+    score_scale = 1.0 / math.sqrt(HEAD_DIM)
+    width = pool_size * PASSAGE
+    keys_flat = pool_keys.reshape(width, HEAD_DIM)
+    values_flat = pool_values.reshape(width, HEAD_DIM)
+    slot_index = jnp.arange(id_table.shape[1])
+    picked = (slot_index[None, :] < count_table[:, None])[:, :, None] & (
+        id_table[:, :, None] == jnp.arange(pool_size)[None, None, :]
+    )
+    usable = jnp.repeat(jnp.any(picked, axis=1).astype(jnp.float32), PASSAGE, axis=1)
+    usable = usable.reshape(-1, blocks_here, width)
+    bias_wide = jnp.tile(row_bias[0], (1, pool_size))
     both_rows = jnp.stack(
         [
             queries.reshape(token_rows, heads_total, HEAD_DIM),
             cotangent.reshape(token_rows, heads_total, HEAD_DIM),
         ]
     ).transpose(2, 0, 1, 3)
-    both_heads = lax.all_to_all(both_rows, "enc", split_axis=0, concat_axis=0, tiled=True)
-    both_out, key_total, value_total, bias_total = attend_all(
-        both_heads, id_table, count_table, pool_keys, pool_values, row_bias
-    )
-    both_back = lax.all_to_all(both_out, "enc", split_axis=0, concat_axis=0, tiled=True)
+    outs, key_parts, value_parts, bias_parts = [], [], [], []
+    for block in range(blocks_here):
+        chunk = both_rows[:, :, block * BLOCK_LEN:(block + 1) * BLOCK_LEN]
+        chunk_heads = lax.all_to_all(chunk, "enc", split_axis=0, concat_axis=0, tiled=True)
+        chunk_out, key_part, value_part, bias_part = attend_all(
+            chunk_heads, usable[:, block:block + 1], keys_flat, values_flat, bias_wide
+        )
+        outs.append(lax.all_to_all(chunk_out, "enc", split_axis=0, concat_axis=0, tiled=True))
+        key_parts.append(key_part)
+        value_parts.append(value_part)
+        bias_parts.append(bias_part)
+    key_total = (score_scale * sum(key_parts[1:], key_parts[0])).astype(jnp.bfloat16)
+    value_total = sum(value_parts[1:], value_parts[0]).astype(jnp.bfloat16)
+    bias_total = sum(bias_parts[1:], bias_parts[0])
+    both_back = jnp.concatenate(outs, axis=2)
     both_back = both_back.transpose(1, 2, 0, 3).reshape((2,) + queries.shape)
     bias_grad = reduce_groups(fold_bias(bias_total[None], rel_bias.shape[1]))
     return (

time: 111 us -> 127 us (1.14)
  blocking collectives: 38.5 us -> 69.3 us
  waiting for transfers between devices: 21 us -> 3.4 us
  Pallas kernels: 14.9 us -> 22.8 us
  starting transfers between devices: 23.3 us -> 18.6 us
  local copies, waits for them, and re-layouts: 10.8 us -> 8.91 us
  other arithmetic: 1.14 us -> 2.95 us
    all_to_all x0 -> x1, blocking collectives: none -> 30.5 us  [local(): lax.all_to_all(chunk, 'enc', split_axis=0, concat_axis=0, tiled=True)]
    all_to_all x2 -> x3, waiting for transfers between devices: 21 us -> 3.4 us  [the longest x2 2.92 us: local(): lax.all_to_all(chunk_out, 'enc', split_axis=0, concat_axis=0, tiled=True)]
    pallas_call x1 -> x2, Pallas kernels: 14.9 us -> 22.8 us  [attend_all(): pl.pallas_call(attend_kernel, grid=grid, in_specs=[pl.BlockSpec((seqs_ste...]
    all_to_all x2 -> x3, starting transfers between devices: 23.3 us -> 18.6 us  [the longest x2 12.6 us: local(): lax.all_to_all(chunk_out, 'enc', split_axis=0, concat_axis=0, tiled=True)]
    unnamed x19 -> x25, local copies, waits for them, and re-layouts: 7.48 us -> 4.63 us
    convert_element_type x1 -> x2, other arithmetic: 0.01 us -> 1.96 us  [the longest x1 1.95 us: local(): value_total = sum(value_parts[1:], value_parts[0]).astype(jnp.bfloat16)]
    slice x0 -> x2, local copies, waits for them, and re-layouts: none -> 1.6 us  [the longest x1 0.86 us: local(): chunk = both_rows[:, :, block * BLOCK_LEN:(block + 1) * BLOCK_LEN]]
  transfers between devices with their start and end apart: 2 -> 3, of which waited for: 1 -> 2; matrix products, arithmetic and copies ran while one was open for 3% -> 5% of each run, Pallas kernels for 0% -> 18%
where the time goes in v5:
time: 127 us
  blocking collectives  69.3 us (55%)
  Pallas kernels  22.8 us (18%)
  starting transfers between devices  18.6 us (15%)
  local copies, waits for them, and re-layouts  8.91 us (7%)
  waiting for transfers between devices  3.4 us (3%)
  other arithmetic  2.95 us (2%)
    psum x2, blocking collectives, reduce_groups(): return lax.psum(lax.psum(part, 'dp'), 'seq')  38.8 us
    all_to_all x1, blocking collectives, local(): lax.all_to_all(chunk, 'enc', split_axis=0, concat_axis=0, tiled=True)  30.5 us
    pallas_call x2, Pallas kernels, attend_all(): pl.pallas_call(attend_kernel, grid=grid, in_specs=[pl.BlockSpec((seqs_ste...  22.8 us
    all_to_all x2, starting transfers between devices, local(): lax.all_to_all(chunk_out, 'enc', split_axis=0, concat_axis=0, tiled=True)  12.6 us
    all_to_all x1, starting transfers between devices, local(): lax.all_to_all(chunk, 'enc', split_axis=0, concat_axis=0, tiled=True)  5.92 us
    unnamed x25, local copies, waits for them, and re-layouts  4.63 us
    all_to_all x2, waiting for transfers between devices, local(): lax.all_to_all(chunk_out, 'enc', split_axis=0, concat_axis=0, tiled=True)  2.92 us
  transfers between devices with their start and end apart: 3, of which 2 were waited for; matrix products, arithmetic and copies ran while one was open for 5% of the time, Pallas kernels for 18%

profile of v5, /device:TPU:16, one launch (start us, length us, event | category | flops | bytes accessed | tf_op | source)
XLA Modules:
  0.0 126.8 jit_solution(2202245891259747537)
XLA Ops:
  0.6 1.4 %copy.24 = bf16[1,128,2048]{1,2,0:T(8,128)(2,1)S(1)} copy(bf16[1,128,2048]{2,1,0:T(8,128)(2,1)} %param.7) | data formatting | bytes 1048576 | tf_op args[0]
  2.0 0.3 copy.26
  2.3 0.3 copy.25
  2.6 0.3 copy.27
  2.9 0.1 maximum_bitcast_fusion
  3.0 0.9 fusion.3
  3.9 30.5 %all_to_all.20.qd_ref = bf16[16,2,64,128]{3,2,1,0:T(8,128)(2,1)} all-to-all(bf16[16,2,64,128]{3,2,1,0:T(8,128)(2,1)S(1)} %get-tuple-element.34), channel_id=1, replica_groups=mesh['dp'=8,'seq'=8,'enc'=16] {'enc'}, dimensions={0} | all-to-all | bytes 1048576 | tf_op jit(solution)/shard_map/all_to_all | solution.py:166
  34.4 5.9 %all-to-all-start = ((bf16[16,2,64,128]{3,2,1,0:T(8,128)(2,1)}), bf16[16,2,64,128]{3,2,1,0:T(8,128)(2,1)S(1)}, u32[]{:S(2)}, u32[]{:S(2)}) async-start(bf16[16,2,64,128]{3,2,1,0:T(8,128)(2,1)} %get-tuple-element.33), calls=%async_computation | async-start | bytes 1048576 | tf_op jit(solution)/shard_map/all_to_all | solution.py:166
  40.4 0.1 lt.20
  40.5 0.1 copy.29
  40.8 0.1 broadcast_in_dim.21
  40.9 0.1 slice_reduce_fusion
  41.1 0.2 reshape.67
  41.3 0.1 broadcast_in_dim.22
  41.6 0.8 copy.38
  42.3 0.7 fusion.4
  43.0 11.4 %shard_map.111 = (bf16[16,2,64,128]{3,2,1,0:T(8,128)(2,1)}, f32[1024,128]{1,0:T(8,128)}, f32[1024,128]{1,0:T(8,128)}, f32[64,128]{1,0:T(8,128)}) custom-call(bf16[16,2,64,128]{3,2,1,0:T(8,128)(2,1)} %all_to_all.20.qd_ref, bf16[1024,128]{1,0:T(8,128)(2,1)} %bitcast.31, bf16[1024,128]{1,0:T(8,128)(2,1)} %bitcast.33, f32[64,1024]{1,0:T(8,128)} %bitcast.24, ...), custom_call_target="tpu_custom_call" | custom-call | tf_op jit(solution)/shard_map/pallas_call | solution.py:99
  54.4 0.5 all-to-all-done.qd_ref
  54.9 6.8 %all-to-all-start.3 = ((bf16[16,2,64,128]{3,2,1,0:T(8,128)(2,1)}), bf16[16,2,64,128]{3,2,1,0:T(8,128)(2,1)S(1)}, u32[]{:S(2)}, u32[]{:S(2)}) async-start(bf16[16,2,64,128]{3,2,1,0:T(8,128)(2,1)} %get-tuple-element.14), calls=%async_computation.3 | async-start | bytes 1048576 | tf_op jit(solution)/shard_map/all_to_all | solution.py:170
  61.7 11.4 %shard_map.110 = (bf16[16,2,64,128]{3,2,1,0:T(8,128)(2,1)}, f32[1024,128]{1,0:T(8,128)}, f32[1024,128]{1,0:T(8,128)}, f32[64,128]{1,0:T(8,128)}) custom-call(bf16[16,2,64,128]{3,2,1,0:T(8,128)(2,1)} %copy-done, bf16[1024,128]{1,0:T(8,128)(2,1)} %bitcast.32, bf16[1024,128]{1,0:T(8,128)(2,1)} %bitcast.34, f32[64,1024]{1,0:T(8,128)} %bitcast.25, ...), custom_call_target="tpu_custom_call" | custom-call | tf_op jit(solution)/shard_map/pallas_call | solution.py:99
  73.1 2.9 %all-to-all-done.3 = bf16[16,2,64,128]{3,2,1,0:T(8,128)(2,1)S(1)} async-done(((bf16[16,2,64,128]{3,2,1,0:T(8,128)(2,1)}), bf16[16,2,64,128]{3,2,1,0:T(8,128)(2,1)S(1)}, u32[]{:S(2)}, u32[]{:S(2)}) %all-to-all-start.3) | async-done | bytes 524320 | tf_op jit(solution)/shard_map/all_to_all | solution.py:170
  76.0 5.9 %all-to-all-start.1 = ((bf16[16,2,64,128]{3,2,1,0:T(8,128)(2,1)}), bf16[16,2,64,128]{3,2,1,0:T(8,128)(2,1)S(1)}, u32[]{:S(2)}, u32[]{:S(2)}) async-start(bf16[16,2,64,128]{3,2,1,0:T(8,128)(2,1)} %get-tuple-element.13), calls=%async_computation.1 | async-start | bytes 1048576 | tf_op jit(solution)/shard_map/all_to_all | solution.py:170
  81.9 0.8 add_bitcast_fusion
  82.7 0.3 reshape.70
  83.0 0.1 pad_reduce_fusion
  83.3 14.2 %psum.14 = f32[1,191]{1,0:T(1,128)S(1)} all-reduce(f32[1,191]{1,0:T(1,128)S(1)} %bitcast.38), channel_id=1, replica_groups=mesh['dp'=8,'seq'=8,'enc'=16] {'dp'}, use_global_device_ids=true, to_apply=%region_2.3 | all-reduce | flops 191 | bytes 1528 | tf_op jit(solution)/shard_map/psum | solution.py:131
  97.4 24.6 %psum.15 = f32[1,191]{1,0:T(1,128)} all-reduce(f32[1,191]{1,0:T(1,128)S(1)} %psum.14), channel_id=1, replica_groups=mesh['dp'=8,'seq'=8,'enc'=16] {'seq'}, use_global_device_ids=true, to_apply=%region_3.4 | all-reduce | flops 191 | bytes 1528 | tf_op jit(solution)/shard_map/psum | solution.py:131
  122.0 2.0 %add_convert_fusion = (bf16[1024,128]{1,0:T(8,128)(2,1)}, bf16[1024,128]{1,0:T(8,128)(2,1)}) fusion(f32[1024,128]{1,0:T(8,128)} %get-tuple-element.17, f32[1024,128]{1,0:T(8,128)S(1)} %copy-done.2, f32[1024,128]{1,0:T(8,128)S(1)} %copy-done.3, f32[1024,128]{1,0:T(8,128)S(1)} %copy-done.1), kind=kLoop, calls=%fused_computation.2 | loop fusion | flops 655360 | bytes 2621440 | tf_op jit(solution)/shard_map/convert_element_type | solution.py:175
  124.2 0.3 copy.33
  124.5 1.0 copy.35
  125.5 0.3 copy.32
  125.7 1.0 copy.34
  (35 shorter events, 0.8 us)
Async XLA Ops:
  0.6 1.7 %copy-start.4 = (bf16[1,128,2048]{2,1,0:T(8,128)(2,1)S(1)}, bf16[1,128,2048]{2,1,0:T(8,128)(2,1)}, u32[]{:S(2)}) copy-start(bf16[1,128,2048]{2,1,0:T(8,128)(2,1)} %param.8) | copy-start | bytes 1572868
  3.9 36.5 %copy-start.7 = (s32[16,2]{0,1:T(2,128)S(1)}, s32[16,2]{0,1:T(2,128)}, u32[]{:S(2)}) copy-start(s32[16,2]{0,1:T(2,128)} %param.11) | copy-start | bytes 388
  3.9 36.7 %copy-start.6 = (s32[16,2,4]{0,2,1:T(4,128)S(1)}, s32[16,2,4]{0,2,1:T(4,128)}, u32[]{:S(2)}) copy-start(s32[16,2,4]{0,2,1:T(4,128)} %param.12) | copy-start | bytes 1540
  3.9 37.0 %copy-start.8 = (f32[1,191]{1,0:T(1,128)S(1)}, f32[1,191]{1,0:T(1,128)}, u32[]{:S(2)}) copy-start(f32[1,191]{1,0:T(1,128)} %param.13) | copy-start | bytes 2296
  34.4 20.5 %all-to-all-start = ((bf16[16,2,64,128]{3,2,1,0:T(8,128)(2,1)}), bf16[16,2,64,128]{3,2,1,0:T(8,128)(2,1)S(1)}, u32[]{:S(2)}, u32[]{:S(2)}) async-start(bf16[16,2,64,128]{3,2,1,0:T(8,128)(2,1)} %get-tuple-element.33), calls=%async_computation | async-start | bytes 1048576 | tf_op jit(solution)/shard_map/all_to_all | solution.py:166
  54.9 6.8 %copy-start = (bf16[16,2,64,128]{3,2,1,0:T(8,128)(2,1)}, bf16[16,2,64,128]{3,2,1,0:T(8,128)(2,1)S(1)}, u32[]{:S(2)}) copy-start(bf16[16,2,64,128]{3,2,1,0:T(8,128)(2,1)S(1)} %all-to-all-done.qd_ref) | copy-start | bytes 1572868
  54.9 21.1 %all-to-all-start.3 = ((bf16[16,2,64,128]{3,2,1,0:T(8,128)(2,1)}), bf16[16,2,64,128]{3,2,1,0:T(8,128)(2,1)S(1)}, u32[]{:S(2)}, u32[]{:S(2)}) async-start(bf16[16,2,64,128]{3,2,1,0:T(8,128)(2,1)} %get-tuple-element.14), calls=%async_computation.3 | async-start | bytes 1048576 | tf_op jit(solution)/shard_map/all_to_all | solution.py:170
  61.7 20.2 %copy-start.5 = (f32[64,128]{1,0:T(8,128)S(1)}, f32[64,128]{1,0:T(8,128)}, u32[]{:S(2)}) copy-start(f32[64,128]{1,0:T(8,128)} %get-tuple-element.20) | copy-start | bytes 98308
  73.1 48.9 %copy-start.1 = (f32[1024,128]{1,0:T(8,128)S(1)}, f32[1024,128]{1,0:T(8,128)}, u32[]{:S(2)}) copy-start(f32[1024,128]{1,0:T(8,128)} %get-tuple-element.16) | copy-start | bytes 1572868
  73.1 48.9 %copy-start.2 = (f32[1024,128]{1,0:T(8,128)S(1)}, f32[1024,128]{1,0:T(8,128)}, u32[]{:S(2)}) copy-start(f32[1024,128]{1,0:T(8,128)} %get-tuple-element.18) | copy-start | bytes 1572868
  73.1 48.9 %copy-start.3 = (f32[1024,128]{1,0:T(8,128)S(1)}, f32[1024,128]{1,0:T(8,128)}, u32[]{:S(2)}) copy-start(f32[1024,128]{1,0:T(8,128)} %get-tuple-element.15) | copy-start | bytes 1572868
  76.0 48.0 %all-to-all-start.1 = ((bf16[16,2,64,128]{3,2,1,0:T(8,128)(2,1)}), bf16[16,2,64,128]{3,2,1,0:T(8,128)(2,1)S(1)}, u32[]{:S(2)}, u32[]{:S(2)}) async-start(bf16[16,2,64,128]{3,2,1,0:T(8,128)(2,1)} %get-tuple-element.13), calls=%async_computation.1 | async-start | bytes 1048576 | tf_op jit(solution)/shard_map/all_to_all | solution.py:170

commit v6 on v4

--- a/solution.py
+++ b/solution.py
@@ -34,16 +34,15 @@
     return flat_rows.reshape(heads_here, BLOCK_LEN, table_width + 1).sum(axis=1)[:, :table_width]
 
 
-def attend_kernel(qd_ref, keys_ref, values_ref, bias_ref, mask_ref, out_ref, key_out, value_out,
+def attend_kernel(qd_ref, keys_ref, values_ref, keys_t_ref, values_t_ref, bias_ref, mask_ref, out_ref, key_out, value_out,
                   bias_out, key_acc, value_acc, bias_acc):
     step = pl.program_id(0)
     score_scale = 1.0 / math.sqrt(HEAD_DIM)
     seqs_here, halves, rows_seq, _ = qd_ref.shape
     blocks_seq = rows_seq // BLOCK_LEN
     rows = seqs_here * rows_seq
-    width = keys_ref.shape[0]
+    width = keys_t_ref.shape[1]
     tile4 = (seqs_here, blocks_seq, BLOCK_LEN, width)
-    contract_last = (((1,), (1,)), ((), ()))
     contract_first = (((0,), (0,)), ((), ()))
 
     @pl.when(step == 0)
@@ -56,7 +55,7 @@
     grad_rows = qd_ref[:, 1].reshape(rows, HEAD_DIM)
     keys = keys_ref[...]
     values = values_ref[...]
-    scores = lax.dot_general(query_rows, keys, contract_last, preferred_element_type=jnp.float32)
+    scores = jnp.dot(query_rows, keys_t_ref[...], preferred_element_type=jnp.float32)
     scores = scores.reshape(tile4) * score_scale + bias_ref[...][None, None]
     usable = mask_ref[...][:, :, None, :] > 0.5
     masked = jnp.where(usable, scores, NEG_FILL)
@@ -68,7 +67,7 @@
     weights = raised * row_scale
     weights_low = weights.astype(jnp.bfloat16).reshape(rows, width)
     context = jnp.dot(weights_low, values, preferred_element_type=jnp.float32)
-    grad_weights = lax.dot_general(grad_rows, values, contract_last, preferred_element_type=jnp.float32)
+    grad_weights = jnp.dot(grad_rows, values_t_ref[...], preferred_element_type=jnp.float32)
     grad_weights = grad_weights.reshape(tile4)
     row_delta = jnp.sum(weights * grad_weights, axis=3, keepdims=True)
     grad_scores = weights * (grad_weights - row_delta)
@@ -76,14 +75,14 @@
     query_grad = score_scale * jnp.dot(scores_low, keys, preferred_element_type=jnp.float32)
     out_ref[:, 0] = context.astype(jnp.bfloat16).reshape(seqs_here, rows_seq, HEAD_DIM)
     out_ref[:, 1] = query_grad.astype(jnp.bfloat16).reshape(seqs_here, rows_seq, HEAD_DIM)
-    key_acc[...] += lax.dot_general(scores_low, query_rows, contract_first, preferred_element_type=jnp.float32)
-    value_acc[...] += lax.dot_general(weights_low, grad_rows, contract_first, preferred_element_type=jnp.float32)
+    key_acc[...] += lax.dot_general(query_rows, scores_low, contract_first, preferred_element_type=jnp.float32)
+    value_acc[...] += lax.dot_general(grad_rows, weights_low, contract_first, preferred_element_type=jnp.float32)
     bias_acc[...] += jnp.sum(grad_scores, axis=(0, 1))
 
     @pl.when(step == pl.num_programs(0) - 1)
     def _():
-        key_out[...] = (score_scale * key_acc[...]).astype(key_out.dtype)
-        value_out[...] = value_acc[...].astype(value_out.dtype)
+        key_out[...] = key_acc[...]
+        value_out[...] = value_acc[...]
         folded = bias_acc[:, 0:PASSAGE]
         for part in range(1, width // PASSAGE):
             folded = folded + bias_acc[:, part * PASSAGE:(part + 1) * PASSAGE]
@@ -104,7 +103,7 @@
     usable = jnp.repeat(jnp.any(picked, axis=1).astype(jnp.float32), PASSAGE, axis=1)
     usable = usable.reshape(seq_total, blocks_seq, width)
     bias_wide = jnp.tile(row_bias[0], (1, pool_size))
-    seqs_step = 2
+    seqs_step = 4
     grid = (seq_total // seqs_step,)
     return pl.pallas_call(
         attend_kernel,
@@ -113,28 +112,30 @@
             pl.BlockSpec((seqs_step, halves, rows_seq, HEAD_DIM), lambda i: (i, 0, 0, 0)),
             pl.BlockSpec((width, HEAD_DIM), lambda i: (0, 0)),
             pl.BlockSpec((width, HEAD_DIM), lambda i: (0, 0)),
+            pl.BlockSpec((HEAD_DIM, width), lambda i: (0, 0)),
+            pl.BlockSpec((HEAD_DIM, width), lambda i: (0, 0)),
             pl.BlockSpec((BLOCK_LEN, width), lambda i: (0, 0)),
             pl.BlockSpec((seqs_step, blocks_seq, width), lambda i: (i, 0, 0)),
         ],
         out_specs=[
             pl.BlockSpec((seqs_step, halves, rows_seq, HEAD_DIM), lambda i: (i, 0, 0, 0)),
-            pl.BlockSpec((width, HEAD_DIM), lambda i: (0, 0)),
-            pl.BlockSpec((width, HEAD_DIM), lambda i: (0, 0)),
+            pl.BlockSpec((HEAD_DIM, width), lambda i: (0, 0)),
+            pl.BlockSpec((HEAD_DIM, width), lambda i: (0, 0)),
             pl.BlockSpec((BLOCK_LEN, PASSAGE), lambda i: (0, 0)),
         ],
         out_shape=[
             jax.ShapeDtypeStruct(both_heads.shape, jnp.bfloat16),
-            jax.ShapeDtypeStruct((width, HEAD_DIM), jnp.bfloat16),
-            jax.ShapeDtypeStruct((width, HEAD_DIM), jnp.bfloat16),
+            jax.ShapeDtypeStruct((HEAD_DIM, width), jnp.float32),
+            jax.ShapeDtypeStruct((HEAD_DIM, width), jnp.float32),
             jax.ShapeDtypeStruct((BLOCK_LEN, PASSAGE), jnp.float32),
         ],
         scratch_shapes=[
-            pltpu.VMEM((width, HEAD_DIM), jnp.float32),
-            pltpu.VMEM((width, HEAD_DIM), jnp.float32),
+            pltpu.VMEM((HEAD_DIM, width), jnp.float32),
+            pltpu.VMEM((HEAD_DIM, width), jnp.float32),
             pltpu.VMEM((BLOCK_LEN, width), jnp.float32),
         ],
         compiler_params=pltpu.CompilerParams(dimension_semantics=("arbitrary",)),
-    )(both_heads, keys_flat, values_flat, bias_wide, usable)
+    )(both_heads, keys_flat, values_flat, keys_flat.T, values_flat.T, bias_wide, usable)
 
 
 def reduce_groups(part):
@@ -153,6 +154,7 @@
     id_table = neighbour_ids.reshape(-1, neighbour_ids.shape[-1])
     count_table = counts.reshape(-1)
     row_bias = bias_rows(rel_bias)
+    score_scale = 1.0 / math.sqrt(HEAD_DIM)
     both_rows = jnp.stack(
         [
             queries.reshape(token_rows, heads_total, HEAD_DIM),
@@ -169,8 +171,8 @@
     return (
         both_back[0],
         both_back[1],
-        key_total.reshape(key_pool.shape),
-        value_total.reshape(value_pool.shape),
+        (score_scale * key_total.T).astype(jnp.bfloat16).reshape(key_pool.shape),
+        value_total.T.astype(jnp.bfloat16).reshape(value_pool.shape),
         bias_grad,
     )
 

time: 111 us -> 110 us (level)
  local copies, waits for them, and re-layouts: 10.8 us -> 14.5 us
  Pallas kernels: 14.9 us -> 11.5 us
  waiting for transfers between devices: 21 us -> 19 us
    pallas_call x1, Pallas kernels: 14.9 us -> 11.5 us  [attend_all(): pl.pallas_call(attend_kernel, grid=grid, in_specs=[pl.BlockSpec((seqs_ste...]
    all_to_all x1, waiting for transfers between devices: 21 us -> 19 us  [local(): lax.all_to_all(both_rows, 'enc', split_axis=0, concat_axis=0, tiled=True)]
    unnamed x19 -> x29, local copies, waits for them, and re-layouts: 7.48 us -> 9.47 us
    another operation x0 -> x2, local copies, waits for them, and re-layouts: none -> 1.7 us  [the longest x1 0.85 us: attend_all(): keys_flat = pool_keys.reshape(width, HEAD_DIM)]
  transfers between devices with their start and end apart: 2 -> 2, of which waited for: 1 -> 1; matrix products, arithmetic and copies ran while one was open for 3% -> 6% of each run, Pallas kernels for 0% -> 0%
where the time goes in v6:
time: 110 us; the launch traced here: 109 us
  blocking collectives  38.5 us (35%)
  starting transfers between devices  23.4 us (21%)
  waiting for transfers between devices  19 us (17%)
  local copies, waits for them, and re-layouts  14.5 us (13%)
  Pallas kernels  11.5 us (10%)
  other arithmetic  1.22 us (1%)
    psum x2, blocking collectives, reduce_groups(): return lax.psum(lax.psum(part, 'dp'), 'seq')  38.5 us
    all_to_all x1, waiting for transfers between devices, local(): lax.all_to_all(both_rows, 'enc', split_axis=0, concat_axis=0, tiled=True)  19 us
    all_to_all x1, starting transfers between devices, local(): lax.all_to_all(both_rows, 'enc', split_axis=0, concat_axis=0, tiled=True)  16.6 us
    pallas_call x1, Pallas kernels, attend_all(): pl.pallas_call(attend_kernel, grid=grid, in_specs=[pl.BlockSpec((seqs_ste...  11.5 us
    unnamed x29, local copies, waits for them, and re-layouts  9.47 us
    all_to_all x1, starting transfers between devices, local(): lax.all_to_all(both_out, 'enc', split_axis=0, concat_axis=0, tiled=True)  6.88 us
  transfers between devices with their start and end apart: 2, of which 1 were waited for; matrix products, arithmetic and copies ran while one was open for 6% of the time, Pallas kernels for 0%

profile of v6, /device:TPU:16, one launch (start us, length us, event | category | flops | bytes accessed | tf_op | source)
XLA Modules:
  0.0 109.0 jit_solution(3904726053220176679)
XLA Ops:
  0.6 1.3 %copy.36 = bf16[1,128,2048]{1,2,0:T(8,128)(2,1)S(1)} copy(bf16[1,128,2048]{2,1,0:T(8,128)(2,1)} %param.7) | data formatting | bytes 1048576 | tf_op args[0]
  2.0 0.3 copy.38
  2.2 0.8 copy-done.5
  3.0 0.3 copy.37
  3.3 0.3 copy.39
  3.6 1.1 maximum_bitcast_fusion
  4.7 16.6 %all-to-all-start = ((bf16[16,2,128,128]{3,2,1,0:T(8,128)(2,1)}), bf16[16,2,128,128]{3,2,1,0:T(8,128)(2,1)S(1)}, u32[]{:S(2)}, u32[]{:S(2)}) async-start(bf16[16,2,128,128]{3,2,1,0:T(8,128)(2,1)} %maximum_bitcast_fusion), calls=%async_computation | async-start | bytes 2097152 | tf_op jit(solution)/shard_map/all_to_all | solution.py:164
  21.4 0.6 copy-done.7
  22.3 0.6 copy-done.9
  22.9 0.1 broadcast_in_dim.21
  23.0 0.1 slice_reduce_fusion
  23.1 0.2 reshape.67
  23.4 0.7 reshape_reshape.11.mask_ref
  24.3 0.8 copy.60
  25.0 0.2 copy-done.1
  25.2 0.8 copy.54
  26.2 0.8 copy.55
  27.0 19.0 %all-to-all-done.qd_ref = bf16[16,2,128,128]{3,2,1,0:T(8,128)(2,1)S(1)} async-done(((bf16[16,2,128,128]{3,2,1,0:T(8,128)(2,1)}), bf16[16,2,128,128]{3,2,1,0:T(8,128)(2,1)S(1)}, u32[]{:S(2)}, u32[]{:S(2)}) %all-to-all-start) | async-done | bytes 1048608 | tf_op jit(solution)/shard_map/all_to_all | solution.py:164
  46.0 1.0 copy-done
  47.0 11.5 %shard_map.110 = (bf16[16,2,128,128]{3,2,1,0:T(8,128)(2,1)}, f32[128,1024]{1,0:T(8,128)}, f32[128,1024]{1,0:T(8,128)}, f32[64,128]{1,0:T(8,128)}) custom-call(bf16[16,2,128,128]{3,2,1,0:T(8,128)(2,1)} %copy-done, bf16[1024,128]{1,0:T(8,128)(2,1)} %bitcast.33, bf16[1024,128]{1,0:T(8,128)(2,1)} %bitcast.35, bf16[128,1024]{1,0:T(8,128)(2,1)} %bitcast.38, ...), custom_call_target="tpu_custom_call" | custom-call | tf_op jit(solution)/shard_map/pallas_call | solution.py:108
  58.5 6.9 %all-to-all-start.1 = ((bf16[16,2,128,128]{3,2,1,0:T(8,128)(2,1)}), bf16[16,2,128,128]{3,2,1,0:T(8,128)(2,1)S(1)}, u32[]{:S(2)}, u32[]{:S(2)}) async-start(bf16[16,2,128,128]{3,2,1,0:T(8,128)(2,1)} %get-tuple-element.9), calls=%async_computation.1 | async-start | bytes 2097152 | tf_op jit(solution)/shard_map/all_to_all | solution.py:168
  65.4 0.3 reshape.70
  65.7 0.1 pad_reduce_fusion
  66.1 0.8 copy.56
  66.9 0.8 copy.57
  67.7 14.1 %psum.14 = f32[1,191]{1,0:T(1,128)S(1)} all-reduce(f32[1,191]{1,0:T(1,128)S(1)} %bitcast.45), channel_id=1, replica_groups=mesh['dp'=8,'seq'=8,'enc'=16] {'dp'}, use_global_device_ids=true, to_apply=%region_2.3 | all-reduce | flops 191 | bytes 1528 | tf_op jit(solution)/shard_map/psum | solution.py:142
  81.9 24.4 %psum.15 = f32[1,191]{1,0:T(1,128)} all-reduce(f32[1,191]{1,0:T(1,128)S(1)} %psum.14), channel_id=1, replica_groups=mesh['dp'=8,'seq'=8,'enc'=16] {'seq'}, use_global_device_ids=true, to_apply=%region_3.4 | all-reduce | flops 191 | bytes 1528 | tf_op jit(solution)/shard_map/psum | solution.py:142
  106.3 0.1 fusion.3
  106.4 0.3 copy.49
  106.7 1.0 copy.51
  107.7 0.3 copy.48
  108.0 1.0 copy.50
  (33 shorter events, 1.0 us)
Async XLA Ops:
  1.9 1.0 copy-start.5
  4.6 16.6 %copy-start.8 = (s32[16,2]{0,1:T(2,128)S(1)}, s32[16,2]{0,1:T(2,128)}, u32[]{:S(2)}) copy-start(s32[16,2]{0,1:T(2,128)} %param.11) | copy-start | bytes 388
  4.7 41.3 %all-to-all-start = ((bf16[16,2,128,128]{3,2,1,0:T(8,128)(2,1)}), bf16[16,2,128,128]{3,2,1,0:T(8,128)(2,1)S(1)}, u32[]{:S(2)}, u32[]{:S(2)}) async-start(bf16[16,2,128,128]{3,2,1,0:T(8,128)(2,1)} %maximum_bitcast_fusion), calls=%async_computation | async-start | bytes 2097152 | tf_op jit(solution)/shard_map/all_to_all | solution.py:164
  21.3 0.7 copy-start.7
  22.2 0.7 copy-start.9
  24.3 1.0 copy-start.1
  25.2 0.9 copy-start.2
  46.0 1.0 copy-start
  58.4 6.9 %copy-start.6 = (f32[64,128]{1,0:T(8,128)S(1)}, f32[64,128]{1,0:T(8,128)}, u32[]{:S(2)}) copy-start(f32[64,128]{1,0:T(8,128)} %get-tuple-element.12) | copy-start | bytes 98308
  58.5 7.5 %copy-start.3 = (f32[128,1024]{1,0:T(8,128)S(1)}, f32[128,1024]{1,0:T(8,128)}, u32[]{:S(2)}) copy-start(f32[128,1024]{1,0:T(8,128)} %get-tuple-element.10) | copy-start | bytes 1572868
  58.5 7.5 %copy-start.4 = (f32[128,1024]{1,0:T(8,128)S(1)}, f32[128,1024]{1,0:T(8,128)}, u32[]{:S(2)}) copy-start(f32[128,1024]{1,0:T(8,128)} %get-tuple-element.11) | copy-start | bytes 1572868
  58.5 47.8 %all-to-all-start.1 = ((bf16[16,2,128,128]{3,2,1,0:T(8,128)(2,1)}), bf16[16,2,128,128]{3,2,1,0:T(8,128)(2,1)S(1)}, u32[]{:S(2)}, u32[]{:S(2)}) async-start(bf16[16,2,128,128]{3,2,1,0:T(8,128)(2,1)} %get-tuple-element.9), calls=%async_computation.1 | async-start | bytes 2097152 | tf_op jit(solution)/shard_map/all_to_all | solution.py:168

commit v7 on v6

--- a/solution.py
+++ b/solution.py
@@ -32,6 +32,20 @@
     flat_rows = padded.reshape(heads_here, BLOCK_LEN * table_width)
     flat_rows = jnp.pad(flat_rows, ((0, 0), (0, BLOCK_LEN)))
     return flat_rows.reshape(heads_here, BLOCK_LEN, table_width + 1).sum(axis=1)[:, :table_width]
+
+
+def split_kernel(query_ref, grad_ref, out_ref):
+    for head in range(out_ref.shape[0]):
+        columns = slice(head * HEAD_DIM, (head + 1) * HEAD_DIM)
+        out_ref[head, 0] = query_ref[:, columns]
+        out_ref[head, 1] = grad_ref[:, columns]
+
+
+def join_kernel(both_ref, context_ref, query_grad_ref):
+    for head in range(both_ref.shape[0]):
+        columns = slice(head * HEAD_DIM, (head + 1) * HEAD_DIM)
+        context_ref[:, columns] = both_ref[head, 0]
+        query_grad_ref[:, columns] = both_ref[head, 1]
 
 
 def attend_kernel(qd_ref, keys_ref, values_ref, keys_t_ref, values_t_ref, bias_ref, mask_ref, out_ref, key_out, value_out,
@@ -81,8 +95,8 @@
 
     @pl.when(step == pl.num_programs(0) - 1)
     def _():
-        key_out[...] = key_acc[...]
-        value_out[...] = value_acc[...]
+        key_out[...] = (score_scale * key_acc[...]).T.astype(key_out.dtype)
+        value_out[...] = value_acc[...].T.astype(value_out.dtype)
         folded = bias_acc[:, 0:PASSAGE]
         for part in range(1, width // PASSAGE):
             folded = folded + bias_acc[:, part * PASSAGE:(part + 1) * PASSAGE]
@@ -119,14 +133,14 @@
         ],
         out_specs=[
             pl.BlockSpec((seqs_step, halves, rows_seq, HEAD_DIM), lambda i: (i, 0, 0, 0)),
-            pl.BlockSpec((HEAD_DIM, width), lambda i: (0, 0)),
-            pl.BlockSpec((HEAD_DIM, width), lambda i: (0, 0)),
+            pl.BlockSpec((width, HEAD_DIM), lambda i: (0, 0)),
+            pl.BlockSpec((width, HEAD_DIM), lambda i: (0, 0)),
             pl.BlockSpec((BLOCK_LEN, PASSAGE), lambda i: (0, 0)),
         ],
         out_shape=[
             jax.ShapeDtypeStruct(both_heads.shape, jnp.bfloat16),
-            jax.ShapeDtypeStruct((HEAD_DIM, width), jnp.float32),
-            jax.ShapeDtypeStruct((HEAD_DIM, width), jnp.float32),
+            jax.ShapeDtypeStruct((width, HEAD_DIM), jnp.bfloat16),
+            jax.ShapeDtypeStruct((width, HEAD_DIM), jnp.bfloat16),
             jax.ShapeDtypeStruct((BLOCK_LEN, PASSAGE), jnp.float32),
         ],
         scratch_shapes=[
@@ -155,24 +169,25 @@
     count_table = counts.reshape(-1)
     row_bias = bias_rows(rel_bias)
     score_scale = 1.0 / math.sqrt(HEAD_DIM)
-    both_rows = jnp.stack(
-        [
-            queries.reshape(token_rows, heads_total, HEAD_DIM),
-            cotangent.reshape(token_rows, heads_total, HEAD_DIM),
-        ]
-    ).transpose(2, 0, 1, 3)
+    both_rows = pl.pallas_call(
+        split_kernel,
+        out_shape=jax.ShapeDtypeStruct((heads_total, 2, token_rows, HEAD_DIM), queries.dtype),
+    )(queries.reshape(token_rows, full_width), cotangent.reshape(token_rows, full_width))
     both_heads = lax.all_to_all(both_rows, "enc", split_axis=0, concat_axis=0, tiled=True)
     both_out, key_total, value_total, bias_total = attend_all(
         both_heads, id_table, count_table, pool_keys, pool_values, row_bias
     )
     both_back = lax.all_to_all(both_out, "enc", split_axis=0, concat_axis=0, tiled=True)
-    both_back = both_back.transpose(1, 2, 0, 3).reshape((2,) + queries.shape)
+    context_rows, query_rows_back = pl.pallas_call(
+        join_kernel,
+        out_shape=[jax.ShapeDtypeStruct((token_rows, full_width), queries.dtype)] * 2,
+    )(both_back)
     bias_grad = reduce_groups(fold_bias(bias_total[None], rel_bias.shape[1]))
     return (
-        both_back[0],
-        both_back[1],
-        (score_scale * key_total.T).astype(jnp.bfloat16).reshape(key_pool.shape),
-        value_total.T.astype(jnp.bfloat16).reshape(value_pool.shape),
+        context_rows.reshape(queries.shape),
+        query_rows_back.reshape(queries.shape),
+        key_total.reshape(key_pool.shape),
+        value_total.reshape(value_pool.shape),
         bias_grad,
     )
 

time: 110 us -> 107 us (0.973)
  local copies, waits for them, and re-layouts: 14.5 us -> 8.23 us
  Pallas kernels: 11.5 us -> 16.3 us
  other arithmetic: 1.22 us -> 0.05 us
    unnamed x29 -> x19, local copies, waits for them, and re-layouts: 9.47 us -> 4.41 us
    pallas_call x0 -> x2, Pallas kernels: none -> 4.86 us  [the longest x1 2.48 us: local(): pl.pallas_call(join_kernel, out_shape=[jax.ShapeDtypeStruct((token_rows,...]
  transfers between devices with their start and end apart: 2 -> 2, of which waited for: 1 -> 1; matrix products, arithmetic and copies ran while one was open for 6% -> 5% of each run, Pallas kernels for 0% -> 0%
where the time goes in v7:
time: 107 us; the launch traced here: 106 us
  blocking collectives  38.5 us (36%)
  starting transfers between devices  23.3 us (22%)
  waiting for transfers between devices  19 us (18%)
  Pallas kernels  16.3 us (15%)
  local copies, waits for them, and re-layouts  8.23 us (8%)
    psum x2, blocking collectives, reduce_groups(): return lax.psum(lax.psum(part, 'dp'), 'seq')  38.5 us
    all_to_all x1, waiting for transfers between devices, local(): lax.all_to_all(both_rows, 'enc', split_axis=0, concat_axis=0, tiled=True)  19 us
    all_to_all x1, starting transfers between devices, local(): lax.all_to_all(both_rows, 'enc', split_axis=0, concat_axis=0, tiled=True)  16.6 us
    pallas_call x1, Pallas kernels, attend_all(): pl.pallas_call(attend_kernel, grid=grid, in_specs=[pl.BlockSpec((seqs_ste...  11.4 us
    all_to_all x1, starting transfers between devices, local(): lax.all_to_all(both_out, 'enc', split_axis=0, concat_axis=0, tiled=True)  6.74 us
    unnamed x19, local copies, waits for them, and re-layouts  4.41 us
    pallas_call x1, Pallas kernels, local(): pl.pallas_call(join_kernel, out_shape=[jax.ShapeDtypeStruct((token_rows,...  2.48 us
    pallas_call x1, Pallas kernels, local(): pl.pallas_call(split_kernel, out_shape=jax.ShapeDtypeStruct((heads_total,...  2.37 us
  transfers between devices with their start and end apart: 2, of which 1 were waited for; matrix products, arithmetic and copies ran while one was open for 5% of the time, Pallas kernels for 0%

profile of v7, /device:TPU:16, one launch (start us, length us, event | category | flops | bytes accessed | tf_op | source)
XLA Modules:
  0.0 106.1 jit_solution(13078230912289660407)
XLA Ops:
  0.6 2.4 %shard_map.110 = bf16[16,2,128,128]{3,2,1,0:T(8,128)(2,1)} custom-call(bf16[128,2048]{1,0:T(8,128)(2,1)} %bitcast.29, bf16[128,2048]{1,0:T(8,128)(2,1)} %bitcast.30), custom_call_target="tpu_custom_call" | custom-call | tf_op jit(solution)/shard_map/pallas_call | solution.py:172
  3.0 16.6 %all-to-all-start = ((bf16[16,2,128,128]{3,2,1,0:T(8,128)(2,1)}), bf16[16,2,128,128]{3,2,1,0:T(8,128)(2,1)S(1)}, u32[]{:S(2)}, u32[]{:S(2)}) async-start(bf16[16,2,128,128]{3,2,1,0:T(8,128)(2,1)} %shard_map.110), calls=%async_computation | async-start | bytes 2097152 | tf_op jit(solution)/shard_map/all_to_all | solution.py:176
  19.6 0.1 copy.26
  19.7 0.1 lt.20
  19.8 0.6 copy-done.5
  20.3 0.1 copy.27
  20.4 0.1 copy.28
  20.6 0.1 copy.29
  20.6 0.6 copy-done.7
  21.3 0.1 broadcast_in_dim.21
  21.4 0.1 slice_reduce_fusion
  21.5 0.2 reshape.76
  21.7 0.1 broadcast_in_dim.22
  21.8 0.7 reshape_reshape.11.mask_ref
  22.5 0.1 slice_bitcast_fusion
  22.6 0.8 copy.36
  23.4 0.2 copy-done.2
  23.6 0.8 copy.32
  24.4 0.1 copy-done.3
  24.5 0.8 copy.33
  25.4 19.0 %all-to-all-done.qd_ref = bf16[16,2,128,128]{3,2,1,0:T(8,128)(2,1)S(1)} async-done(((bf16[16,2,128,128]{3,2,1,0:T(8,128)(2,1)}), bf16[16,2,128,128]{3,2,1,0:T(8,128)(2,1)S(1)}, u32[]{:S(2)}, u32[]{:S(2)}) %all-to-all-start) | async-done | bytes 1048608 | tf_op jit(solution)/shard_map/all_to_all | solution.py:176
  44.3 1.0 copy-done
  45.3 11.4 %shard_map.111 = (bf16[16,2,128,128]{3,2,1,0:T(8,128)(2,1)}, bf16[1024,128]{1,0:T(8,128)(2,1)}, bf16[1024,128]{1,0:T(8,128)(2,1)}, f32[64,128]{1,0:T(8,128)}) custom-call(bf16[16,2,128,128]{3,2,1,0:T(8,128)(2,1)} %copy-done, bf16[1024,128]{1,0:T(8,128)(2,1)} %bitcast.21, bf16[1024,128]{1,0:T(8,128)(2,1)} %bitcast.23, bf16[128,1024]{1,0:T(8,128)(2,1)} %bitcast.26, ...), custom_call_target="tpu_custom_call" | custom-call | tf_op jit(solution)/shard_map/pallas_call | solution.py:122
  56.8 6.7 %all-to-all-start.1 = ((bf16[16,2,128,128]{3,2,1,0:T(8,128)(2,1)}), bf16[16,2,128,128]{3,2,1,0:T(8,128)(2,1)S(1)}, u32[]{:S(2)}, u32[]{:S(2)}) async-start(bf16[16,2,128,128]{3,2,1,0:T(8,128)(2,1)} %get-tuple-element.11), calls=%async_computation.1 | async-start | bytes 2097152 | tf_op jit(solution)/shard_map/all_to_all | solution.py:180
  63.5 0.1 pad.13
  63.6 0.3 reshape.81
  63.9 0.1 pad_reduce_fusion
  64.0 0.1 reshape.82
  64.1 14.2 %psum.14 = f32[1,191]{1,0:T(1,128)S(1)} all-reduce(f32[1,191]{1,0:T(1,128)S(1)} %bitcast.33), channel_id=1, replica_groups=mesh['dp'=8,'seq'=8,'enc'=16] {'dp'}, use_global_device_ids=true, to_apply=%region_2.3 | all-reduce | flops 191 | bytes 1528 | tf_op jit(solution)/shard_map/psum | solution.py:156
  78.3 24.4 %psum.15 = f32[1,191]{1,0:T(1,128)} all-reduce(f32[1,191]{1,0:T(1,128)S(1)} %psum.14), channel_id=1, replica_groups=mesh['dp'=8,'seq'=8,'enc'=16] {'seq'}, use_global_device_ids=true, to_apply=%region_3.4 | all-reduce | flops 191 | bytes 1528 | tf_op jit(solution)/shard_map/psum | solution.py:156
  102.7 1.0 copy-done.1
  103.7 2.5 %shard_map.112 = (bf16[128,2048]{1,0:T(8,128)(2,1)}, bf16[128,2048]{1,0:T(8,128)(2,1)}) custom-call(bf16[16,2,128,128]{3,2,1,0:T(8,128)(2,1)} %copy-done.1), custom_call_target="tpu_custom_call" | custom-call | tf_op jit(solution)/shard_map/pallas_call | solution.py:181
  (18 shorter events, 0.1 us)
Async XLA Ops:
  3.0 16.6 %copy-start.6 = (s32[16,2]{0,1:T(2,128)S(1)}, s32[16,2]{0,1:T(2,128)}, u32[]{:S(2)}) copy-start(s32[16,2]{0,1:T(2,128)} %param.11) | copy-start | bytes 388
  3.0 41.3 %all-to-all-start = ((bf16[16,2,128,128]{3,2,1,0:T(8,128)(2,1)}), bf16[16,2,128,128]{3,2,1,0:T(8,128)(2,1)S(1)}, u32[]{:S(2)}, u32[]{:S(2)}) async-start(bf16[16,2,128,128]{3,2,1,0:T(8,128)(2,1)} %shard_map.110), calls=%async_computation | async-start | bytes 2097152 | tf_op jit(solution)/shard_map/all_to_all | solution.py:176
  19.7 0.7 copy-start.5
  20.6 0.7 copy-start.7
  22.6 1.0 copy-start.2
  23.6 0.9 copy-start.3
  44.3 1.0 copy-start
  56.8 6.8 %copy-start.4 = (f32[64,128]{1,0:T(8,128)S(1)}, f32[64,128]{1,0:T(8,128)}, u32[]{:S(2)}) copy-start(f32[64,128]{1,0:T(8,128)} %get-tuple-element.16) | copy-start | bytes 98308
  56.8 45.9 %all-to-all-start.1 = ((bf16[16,2,128,128]{3,2,1,0:T(8,128)(2,1)}), bf16[16,2,128,128]{3,2,1,0:T(8,128)(2,1)S(1)}, u32[]{:S(2)}, u32[]{:S(2)}) async-start(bf16[16,2,128,128]{3,2,1,0:T(8,128)(2,1)} %get-tuple-element.11), calls=%async_computation.1 | async-start | bytes 2097152 | tf_op jit(solution)/shard_map/all_to_all | solution.py:180
  102.7 1.0 copy-start.1

commit v8 on v7

--- a/solution.py
+++ b/solution.py
@@ -39,13 +39,6 @@
         columns = slice(head * HEAD_DIM, (head + 1) * HEAD_DIM)
         out_ref[head, 0] = query_ref[:, columns]
         out_ref[head, 1] = grad_ref[:, columns]
-
-
-def join_kernel(both_ref, context_ref, query_grad_ref):
-    for head in range(both_ref.shape[0]):
-        columns = slice(head * HEAD_DIM, (head + 1) * HEAD_DIM)
-        context_ref[:, columns] = both_ref[head, 0]
-        query_grad_ref[:, columns] = both_ref[head, 1]
 
 
 def attend_kernel(qd_ref, keys_ref, values_ref, keys_t_ref, values_t_ref, bias_ref, mask_ref, out_ref, key_out, value_out,
@@ -178,14 +171,11 @@
         both_heads, id_table, count_table, pool_keys, pool_values, row_bias
     )
     both_back = lax.all_to_all(both_out, "enc", split_axis=0, concat_axis=0, tiled=True)
-    context_rows, query_rows_back = pl.pallas_call(
-        join_kernel,
-        out_shape=[jax.ShapeDtypeStruct((token_rows, full_width), queries.dtype)] * 2,
-    )(both_back)
+    both_back = both_back.transpose(1, 2, 0, 3).reshape((2,) + queries.shape)
     bias_grad = reduce_groups(fold_bias(bias_total[None], rel_bias.shape[1]))
     return (
-        context_rows.reshape(queries.shape),
-        query_rows_back.reshape(queries.shape),
+        both_back[0],
+        both_back[1],
         key_total.reshape(key_pool.shape),
         value_total.reshape(value_pool.shape),
         bias_grad,

time: 107 us -> 106 us (level)
  Pallas kernels: 16.3 us -> 13.8 us
  local copies, waits for them, and re-layouts: 8.23 us -> 9.93 us
    pallas_call x1 -> x0, Pallas kernels: 2.48 us -> none  [local(): pl.pallas_call(join_kernel, out_shape=[jax.ShapeDtypeStruct((token_rows,...]
where the time goes in v8:
time: 106 us; the launch traced here: 105 us
  blocking collectives  38.5 us (36%)
  starting transfers between devices  23.3 us (22%)
  waiting for transfers between devices  19 us (18%)
  Pallas kernels  13.8 us (13%)
  local copies, waits for them, and re-layouts  9.93 us (9%)
    psum x2, blocking collectives, reduce_groups(): return lax.psum(lax.psum(part, 'dp'), 'seq')  38.5 us
    all_to_all x1, waiting for transfers between devices, local(): lax.all_to_all(both_rows, 'enc', split_axis=0, concat_axis=0, tiled=True)  19 us
    all_to_all x1, starting transfers between devices, local(): lax.all_to_all(both_rows, 'enc', split_axis=0, concat_axis=0, tiled=True)  16.6 us
    pallas_call x1, Pallas kernels, attend_all(): pl.pallas_call(attend_kernel, grid=grid, in_specs=[pl.BlockSpec((seqs_ste...  11.4 us
    all_to_all x1, starting transfers between devices, local(): lax.all_to_all(both_out, 'enc', split_axis=0, concat_axis=0, tiled=True)  6.74 us
    unnamed x19, local copies, waits for them, and re-layouts  5.44 us
    pallas_call x1, Pallas kernels, local(): pl.pallas_call(split_kernel, out_shape=jax.ShapeDtypeStruct((heads_total,...  2.37 us
  transfers between devices with their start and end apart: 2, of which 1 were waited for; matrix products, arithmetic and copies ran while one was open for 5% of the time, Pallas kernels for 0%

profile of v8, /device:TPU:16, one launch (start us, length us, event | category | flops | bytes accessed | tf_op | source)
XLA Modules:
  0.0 105.4 jit_solution(10573348666860356108)
XLA Ops:
  0.6 2.4 %shard_map.110 = bf16[16,2,128,128]{3,2,1,0:T(8,128)(2,1)} custom-call(bf16[128,2048]{1,0:T(8,128)(2,1)} %bitcast.33, bf16[128,2048]{1,0:T(8,128)(2,1)} %bitcast.34), custom_call_target="tpu_custom_call" | custom-call | tf_op jit(solution)/shard_map/pallas_call | solution.py:165
  3.0 16.6 %all-to-all-start = ((bf16[16,2,128,128]{3,2,1,0:T(8,128)(2,1)}), bf16[16,2,128,128]{3,2,1,0:T(8,128)(2,1)S(1)}, u32[]{:S(2)}, u32[]{:S(2)}) async-start(bf16[16,2,128,128]{3,2,1,0:T(8,128)(2,1)} %shard_map.110), calls=%async_computation | async-start | bytes 2097152 | tf_op jit(solution)/shard_map/all_to_all | solution.py:169
  19.6 0.1 copy.30
  19.7 0.1 lt.20
  19.8 0.6 copy-done.4
  20.3 0.1 copy.31
  20.4 0.1 copy.32
  20.6 0.6 copy-done.6
  21.3 0.1 broadcast_in_dim.21
  21.4 0.1 slice_reduce_fusion
  21.5 0.2 reshape.75
  21.7 0.1 broadcast_in_dim.22
  21.8 0.7 reshape_reshape.11.mask_ref
  22.6 0.8 copy.44
  23.4 0.2 copy-done.1
  23.6 0.8 copy.40
  24.4 0.1 copy-done.2
  24.5 0.8 copy.41
  25.4 19.0 %all-to-all-done.qd_ref = bf16[16,2,128,128]{3,2,1,0:T(8,128)(2,1)S(1)} async-done(((bf16[16,2,128,128]{3,2,1,0:T(8,128)(2,1)}), bf16[16,2,128,128]{3,2,1,0:T(8,128)(2,1)S(1)}, u32[]{:S(2)}, u32[]{:S(2)}) %all-to-all-start) | async-done | bytes 1048608 | tf_op jit(solution)/shard_map/all_to_all | solution.py:169
  44.3 1.0 copy-done
  45.3 11.4 %shard_map.111 = (bf16[16,2,128,128]{3,2,1,0:T(8,128)(2,1)}, bf16[1024,128]{1,0:T(8,128)(2,1)}, bf16[1024,128]{1,0:T(8,128)(2,1)}, f32[64,128]{1,0:T(8,128)}) custom-call(bf16[16,2,128,128]{3,2,1,0:T(8,128)(2,1)} %copy-done, bf16[1024,128]{1,0:T(8,128)(2,1)} %bitcast.25, bf16[1024,128]{1,0:T(8,128)(2,1)} %bitcast.27, bf16[128,1024]{1,0:T(8,128)(2,1)} %bitcast.30, ...), custom_call_target="tpu_custom_call" | custom-call | tf_op jit(solution)/shard_map/pallas_call | solution.py:115
  56.8 6.7 %all-to-all-start.1 = ((bf16[16,2,128,128]{3,2,1,0:T(8,128)(2,1)}), bf16[16,2,128,128]{3,2,1,0:T(8,128)(2,1)S(1)}, u32[]{:S(2)}, u32[]{:S(2)}) async-start(bf16[16,2,128,128]{3,2,1,0:T(8,128)(2,1)} %get-tuple-element.9), calls=%async_computation.1 | async-start | bytes 2097152 | tf_op jit(solution)/shard_map/all_to_all | solution.py:173
  63.5 0.1 pad.13
  63.6 0.3 reshape.78
  63.9 0.1 pad_reduce_fusion
  64.1 14.2 %psum.14 = f32[1,191]{1,0:T(1,128)S(1)} all-reduce(f32[1,191]{1,0:T(1,128)S(1)} %bitcast.37), channel_id=1, replica_groups=mesh['dp'=8,'seq'=8,'enc'=16] {'dp'}, use_global_device_ids=true, to_apply=%region_2.3 | all-reduce | flops 191 | bytes 1528 | tf_op jit(solution)/shard_map/psum | solution.py:149
  78.3 24.4 %psum.15 = f32[1,191]{1,0:T(1,128)} all-reduce(f32[1,191]{1,0:T(1,128)S(1)} %psum.14), channel_id=1, replica_groups=mesh['dp'=8,'seq'=8,'enc'=16] {'seq'}, use_global_device_ids=true, to_apply=%region_3.4 | all-reduce | flops 191 | bytes 1528 | tf_op jit(solution)/shard_map/psum | solution.py:149
  102.7 0.1 fusion.2
  102.8 0.3 copy.37
  103.1 1.0 copy.39
  104.1 0.3 copy.36
  104.4 1.0 copy.38
  (20 shorter events, 0.3 us)
Async XLA Ops:
  3.0 16.6 %copy-start.5 = (s32[16,2]{0,1:T(2,128)S(1)}, s32[16,2]{0,1:T(2,128)}, u32[]{:S(2)}) copy-start(s32[16,2]{0,1:T(2,128)} %param.11) | copy-start | bytes 388
  3.0 41.3 %all-to-all-start = ((bf16[16,2,128,128]{3,2,1,0:T(8,128)(2,1)}), bf16[16,2,128,128]{3,2,1,0:T(8,128)(2,1)S(1)}, u32[]{:S(2)}, u32[]{:S(2)}) async-start(bf16[16,2,128,128]{3,2,1,0:T(8,128)(2,1)} %shard_map.110), calls=%async_computation | async-start | bytes 2097152 | tf_op jit(solution)/shard_map/all_to_all | solution.py:169
  19.7 0.7 copy-start.4
  20.6 0.7 copy-start.6
  22.6 1.0 copy-start.1
  23.6 0.9 copy-start.2
  44.3 1.0 copy-start
  56.8 6.8 %copy-start.3 = (f32[64,128]{1,0:T(8,128)S(1)}, f32[64,128]{1,0:T(8,128)}, u32[]{:S(2)}) copy-start(f32[64,128]{1,0:T(8,128)} %get-tuple-element.12) | copy-start | bytes 98308
  56.8 45.9 %all-to-all-start.1 = ((bf16[16,2,128,128]{3,2,1,0:T(8,128)(2,1)}), bf16[16,2,128,128]{3,2,1,0:T(8,128)(2,1)S(1)}, u32[]{:S(2)}, u32[]{:S(2)}) async-start(bf16[16,2,128,128]{3,2,1,0:T(8,128)(2,1)} %get-tuple-element.9), calls=%async_computation.1 | async-start | bytes 2097152 | tf_op jit(solution)/shard_map/all_to_all | solution.py:173

commit v9 on v8

--- a/solution.py
+++ b/solution.py
@@ -146,7 +146,7 @@
 
 
 def reduce_groups(part):
-    return lax.psum(lax.psum(part, "dp"), "seq")
+    return lax.psum(lax.psum(part, "seq"), "dp")
 
 
 def local(queries, cotangent, key_pool, value_pool, counts, neighbour_ids, rel_bias):

time: 106 us -> 106 us (level)
  no operation moved by 1% of the time
where the time goes in v9:
time: 106 us; the launch traced here: 105 us
  blocking collectives  38.5 us (36%)
  starting transfers between devices  23.3 us (22%)
  waiting for transfers between devices  19 us (18%)
  Pallas kernels  13.8 us (13%)
  local copies, waits for them, and re-layouts  9.93 us (9%)
    psum x2, blocking collectives, reduce_groups(): return lax.psum(lax.psum(part, 'seq'), 'dp')  38.5 us
    all_to_all x1, waiting for transfers between devices, local(): lax.all_to_all(both_rows, 'enc', split_axis=0, concat_axis=0, tiled=True)  19 us
    all_to_all x1, starting transfers between devices, local(): lax.all_to_all(both_rows, 'enc', split_axis=0, concat_axis=0, tiled=True)  16.6 us
    pallas_call x1, Pallas kernels, attend_all(): pl.pallas_call(attend_kernel, grid=grid, in_specs=[pl.BlockSpec((seqs_ste...  11.4 us
    all_to_all x1, starting transfers between devices, local(): lax.all_to_all(both_out, 'enc', split_axis=0, concat_axis=0, tiled=True)  6.74 us
    unnamed x19, local copies, waits for them, and re-layouts  5.44 us
    pallas_call x1, Pallas kernels, local(): pl.pallas_call(split_kernel, out_shape=jax.ShapeDtypeStruct((heads_total,...  2.37 us
  transfers between devices with their start and end apart: 2, of which 1 were waited for; matrix products, arithmetic and copies ran while one was open for 5% of the time, Pallas kernels for 0%

profile of v9, /device:TPU:16, one launch (start us, length us, event | category | flops | bytes accessed | tf_op | source)
XLA Modules:
  0.0 105.4 jit_solution(2292492900436078168)
XLA Ops:
  0.6 2.4 %shard_map.110 = bf16[16,2,128,128]{3,2,1,0:T(8,128)(2,1)} custom-call(bf16[128,2048]{1,0:T(8,128)(2,1)} %bitcast.33, bf16[128,2048]{1,0:T(8,128)(2,1)} %bitcast.34), custom_call_target="tpu_custom_call" | custom-call | tf_op jit(solution)/shard_map/pallas_call | solution.py:165
  3.0 16.6 %all-to-all-start = ((bf16[16,2,128,128]{3,2,1,0:T(8,128)(2,1)}), bf16[16,2,128,128]{3,2,1,0:T(8,128)(2,1)S(1)}, u32[]{:S(2)}, u32[]{:S(2)}) async-start(bf16[16,2,128,128]{3,2,1,0:T(8,128)(2,1)} %shard_map.110), calls=%async_computation | async-start | bytes 2097152 | tf_op jit(solution)/shard_map/all_to_all | solution.py:169
  19.6 0.1 copy.30
  19.7 0.1 lt.20
  19.8 0.6 copy-done.4
  20.3 0.1 copy.31
  20.4 0.1 copy.32
  20.6 0.6 copy-done.6
  21.3 0.1 broadcast_in_dim.21
  21.4 0.1 slice_reduce_fusion
  21.5 0.2 reshape.75
  21.7 0.1 broadcast_in_dim.22
  21.8 0.7 reshape_reshape.11.mask_ref
  22.6 0.8 copy.44
  23.4 0.2 copy-done.1
  23.6 0.8 copy.40
  24.4 0.1 copy-done.2
  24.5 0.8 copy.41
  25.4 19.0 %all-to-all-done.qd_ref = bf16[16,2,128,128]{3,2,1,0:T(8,128)(2,1)S(1)} async-done(((bf16[16,2,128,128]{3,2,1,0:T(8,128)(2,1)}), bf16[16,2,128,128]{3,2,1,0:T(8,128)(2,1)S(1)}, u32[]{:S(2)}, u32[]{:S(2)}) %all-to-all-start) | async-done | bytes 1048608 | tf_op jit(solution)/shard_map/all_to_all | solution.py:169
  44.3 1.0 copy-done
  45.3 11.4 %shard_map.111 = (bf16[16,2,128,128]{3,2,1,0:T(8,128)(2,1)}, bf16[1024,128]{1,0:T(8,128)(2,1)}, bf16[1024,128]{1,0:T(8,128)(2,1)}, f32[64,128]{1,0:T(8,128)}) custom-call(bf16[16,2,128,128]{3,2,1,0:T(8,128)(2,1)} %copy-done, bf16[1024,128]{1,0:T(8,128)(2,1)} %bitcast.25, bf16[1024,128]{1,0:T(8,128)(2,1)} %bitcast.27, bf16[128,1024]{1,0:T(8,128)(2,1)} %bitcast.30, ...), custom_call_target="tpu_custom_call" | custom-call | tf_op jit(solution)/shard_map/pallas_call | solution.py:115
  56.8 6.7 %all-to-all-start.1 = ((bf16[16,2,128,128]{3,2,1,0:T(8,128)(2,1)}), bf16[16,2,128,128]{3,2,1,0:T(8,128)(2,1)S(1)}, u32[]{:S(2)}, u32[]{:S(2)}) async-start(bf16[16,2,128,128]{3,2,1,0:T(8,128)(2,1)} %get-tuple-element.9), calls=%async_computation.1 | async-start | bytes 2097152 | tf_op jit(solution)/shard_map/all_to_all | solution.py:173
  63.5 0.1 pad.13
  63.6 0.3 reshape.78
  63.9 0.1 pad_reduce_fusion
  64.1 21.0 %psum.14 = f32[1,191]{1,0:T(1,128)S(1)} all-reduce(f32[1,191]{1,0:T(1,128)S(1)} %bitcast.37), channel_id=1, replica_groups=mesh['dp'=8,'seq'=8,'enc'=16] {'seq'}, use_global_device_ids=true, to_apply=%region_2.3 | all-reduce | flops 191 | bytes 1528 | tf_op jit(solution)/shard_map/psum | solution.py:149
  85.1 17.6 %psum.15 = f32[1,191]{1,0:T(1,128)} all-reduce(f32[1,191]{1,0:T(1,128)S(1)} %psum.14), channel_id=1, replica_groups=mesh['dp'=8,'seq'=8,'enc'=16] {'dp'}, use_global_device_ids=true, to_apply=%region_3.4 | all-reduce | flops 191 | bytes 1528 | tf_op jit(solution)/shard_map/psum | solution.py:149
  102.7 0.1 fusion.2
  102.8 0.3 copy.37
  103.1 1.0 copy.39
  104.1 0.3 copy.36
  104.4 1.0 copy.38
  (20 shorter events, 0.3 us)
Async XLA Ops:
  3.0 16.6 %copy-start.5 = (s32[16,2]{0,1:T(2,128)S(1)}, s32[16,2]{0,1:T(2,128)}, u32[]{:S(2)}) copy-start(s32[16,2]{0,1:T(2,128)} %param.11) | copy-start | bytes 388
  3.0 41.3 %all-to-all-start = ((bf16[16,2,128,128]{3,2,1,0:T(8,128)(2,1)}), bf16[16,2,128,128]{3,2,1,0:T(8,128)(2,1)S(1)}, u32[]{:S(2)}, u32[]{:S(2)}) async-start(bf16[16,2,128,128]{3,2,1,0:T(8,128)(2,1)} %shard_map.110), calls=%async_computation | async-start | bytes 2097152 | tf_op jit(solution)/shard_map/all_to_all | solution.py:169
  19.7 0.7 copy-start.4
  20.6 0.7 copy-start.6
  22.6 1.0 copy-start.1
  23.6 0.9 copy-start.2
  44.3 1.0 copy-start
  56.8 6.8 %copy-start.3 = (f32[64,128]{1,0:T(8,128)S(1)}, f32[64,128]{1,0:T(8,128)}, u32[]{:S(2)}) copy-start(f32[64,128]{1,0:T(8,128)} %get-tuple-element.12) | copy-start | bytes 98308
  56.8 45.9 %all-to-all-start.1 = ((bf16[16,2,128,128]{3,2,1,0:T(8,128)(2,1)}), bf16[16,2,128,128]{3,2,1,0:T(8,128)(2,1)S(1)}, u32[]{:S(2)}, u32[]{:S(2)}) async-start(bf16[16,2,128,128]{3,2,1,0:T(8,128)(2,1)} %get-tuple-element.9), calls=%async_computation.1 | async-start | bytes 2097152 | tf_op jit(solution)/shard_map/all_to_all | solution.py:173

commit v10 on v9

--- a/solution.py
+++ b/solution.py
@@ -110,7 +110,7 @@
     usable = jnp.repeat(jnp.any(picked, axis=1).astype(jnp.float32), PASSAGE, axis=1)
     usable = usable.reshape(seq_total, blocks_seq, width)
     bias_wide = jnp.tile(row_bias[0], (1, pool_size))
-    seqs_step = 4
+    seqs_step = 8
     grid = (seq_total // seqs_step,)
     return pl.pallas_call(
         attend_kernel,

time: 106 us -> 105 us (level)
  no operation moved by 1% of the time
where the time goes in v10:
time: 105 us; the launch traced here: 104 us
  blocking collectives  38.5 us (37%)
  starting transfers between devices  23.3 us (22%)
  waiting for transfers between devices  19 us (18%)
  Pallas kernels  12.9 us (12%)
  local copies, waits for them, and re-layouts  9.93 us (9%)
    psum x2, blocking collectives, reduce_groups(): return lax.psum(lax.psum(part, 'seq'), 'dp')  38.5 us
    all_to_all x1, waiting for transfers between devices, local(): lax.all_to_all(both_rows, 'enc', split_axis=0, concat_axis=0, tiled=True)  19 us
    all_to_all x1, starting transfers between devices, local(): lax.all_to_all(both_rows, 'enc', split_axis=0, concat_axis=0, tiled=True)  16.6 us
    pallas_call x1, Pallas kernels, attend_all(): pl.pallas_call(attend_kernel, grid=grid, in_specs=[pl.BlockSpec((seqs_ste...  10.5 us
    all_to_all x1, starting transfers between devices, local(): lax.all_to_all(both_out, 'enc', split_axis=0, concat_axis=0, tiled=True)  6.74 us
    unnamed x19, local copies, waits for them, and re-layouts  5.44 us
    pallas_call x1, Pallas kernels, local(): pl.pallas_call(split_kernel, out_shape=jax.ShapeDtypeStruct((heads_total,...  2.37 us
  transfers between devices with their start and end apart: 2, of which 1 were waited for; matrix products, arithmetic and copies ran while one was open for 5% of the time, Pallas kernels for 0%

profile of v10, /device:TPU:16, one launch (start us, length us, event | category | flops | bytes accessed | tf_op | source)
XLA Modules:
  0.0 104.5 jit_solution(18268580047551181374)
XLA Ops:
  0.6 2.4 %shard_map.110 = bf16[16,2,128,128]{3,2,1,0:T(8,128)(2,1)} custom-call(bf16[128,2048]{1,0:T(8,128)(2,1)} %bitcast.33, bf16[128,2048]{1,0:T(8,128)(2,1)} %bitcast.34), custom_call_target="tpu_custom_call" | custom-call | tf_op jit(solution)/shard_map/pallas_call | solution.py:165
  3.0 16.6 %all-to-all-start = ((bf16[16,2,128,128]{3,2,1,0:T(8,128)(2,1)}), bf16[16,2,128,128]{3,2,1,0:T(8,128)(2,1)S(1)}, u32[]{:S(2)}, u32[]{:S(2)}) async-start(bf16[16,2,128,128]{3,2,1,0:T(8,128)(2,1)} %shard_map.110), calls=%async_computation | async-start | bytes 2097152 | tf_op jit(solution)/shard_map/all_to_all | solution.py:169
  19.6 0.1 copy.30
  19.7 0.1 lt.20
  19.8 0.6 copy-done.4
  20.3 0.1 copy.31
  20.4 0.1 copy.32
  20.6 0.6 copy-done.6
  21.3 0.1 broadcast_in_dim.21
  21.4 0.1 slice_reduce_fusion
  21.5 0.2 reshape.75
  21.7 0.1 broadcast_in_dim.22
  21.8 0.7 reshape_reshape.11.mask_ref
  22.6 0.8 copy.44
  23.4 0.2 copy-done.1
  23.6 0.8 copy.40
  24.4 0.1 copy-done.2
  24.5 0.8 copy.41
  25.4 19.0 %all-to-all-done.qd_ref = bf16[16,2,128,128]{3,2,1,0:T(8,128)(2,1)S(1)} async-done(((bf16[16,2,128,128]{3,2,1,0:T(8,128)(2,1)}), bf16[16,2,128,128]{3,2,1,0:T(8,128)(2,1)S(1)}, u32[]{:S(2)}, u32[]{:S(2)}) %all-to-all-start) | async-done | bytes 1048608 | tf_op jit(solution)/shard_map/all_to_all | solution.py:169
  44.3 1.0 copy-done
  45.3 10.5 %shard_map.111 = (bf16[16,2,128,128]{3,2,1,0:T(8,128)(2,1)}, bf16[1024,128]{1,0:T(8,128)(2,1)}, bf16[1024,128]{1,0:T(8,128)(2,1)}, f32[64,128]{1,0:T(8,128)}) custom-call(bf16[16,2,128,128]{3,2,1,0:T(8,128)(2,1)} %copy-done, bf16[1024,128]{1,0:T(8,128)(2,1)} %bitcast.25, bf16[1024,128]{1,0:T(8,128)(2,1)} %bitcast.27, bf16[128,1024]{1,0:T(8,128)(2,1)} %bitcast.30, ...), custom_call_target="tpu_custom_call" | custom-call | tf_op jit(solution)/shard_map/pallas_call | solution.py:115
  55.9 6.7 %all-to-all-start.1 = ((bf16[16,2,128,128]{3,2,1,0:T(8,128)(2,1)}), bf16[16,2,128,128]{3,2,1,0:T(8,128)(2,1)S(1)}, u32[]{:S(2)}, u32[]{:S(2)}) async-start(bf16[16,2,128,128]{3,2,1,0:T(8,128)(2,1)} %get-tuple-element.9), calls=%async_computation.1 | async-start | bytes 2097152 | tf_op jit(solution)/shard_map/all_to_all | solution.py:173
  62.6 0.1 pad.13
  62.7 0.3 reshape.78
  63.0 0.1 pad_reduce_fusion
  63.2 21.0 %psum.14 = f32[1,191]{1,0:T(1,128)S(1)} all-reduce(f32[1,191]{1,0:T(1,128)S(1)} %bitcast.37), channel_id=1, replica_groups=mesh['dp'=8,'seq'=8,'enc'=16] {'seq'}, use_global_device_ids=true, to_apply=%region_2.3 | all-reduce | flops 191 | bytes 1528 | tf_op jit(solution)/shard_map/psum | solution.py:149
  84.2 17.6 %psum.15 = f32[1,191]{1,0:T(1,128)} all-reduce(f32[1,191]{1,0:T(1,128)S(1)} %psum.14), channel_id=1, replica_groups=mesh['dp'=8,'seq'=8,'enc'=16] {'dp'}, use_global_device_ids=true, to_apply=%region_3.4 | all-reduce | flops 191 | bytes 1528 | tf_op jit(solution)/shard_map/psum | solution.py:149
  101.8 0.1 fusion.2
  101.9 0.3 copy.37
  102.1 1.0 copy.39
  103.2 0.3 copy.36
  103.4 1.0 copy.38
  (20 shorter events, 0.3 us)
Async XLA Ops:
  3.0 16.6 %copy-start.5 = (s32[16,2]{0,1:T(2,128)S(1)}, s32[16,2]{0,1:T(2,128)}, u32[]{:S(2)}) copy-start(s32[16,2]{0,1:T(2,128)} %param.11) | copy-start | bytes 388
  3.0 41.3 %all-to-all-start = ((bf16[16,2,128,128]{3,2,1,0:T(8,128)(2,1)}), bf16[16,2,128,128]{3,2,1,0:T(8,128)(2,1)S(1)}, u32[]{:S(2)}, u32[]{:S(2)}) async-start(bf16[16,2,128,128]{3,2,1,0:T(8,128)(2,1)} %shard_map.110), calls=%async_computation | async-start | bytes 2097152 | tf_op jit(solution)/shard_map/all_to_all | solution.py:169
  19.7 0.7 copy-start.4
  20.6 0.7 copy-start.6
  22.6 1.0 copy-start.1
  23.6 0.9 copy-start.2
  44.3 1.0 copy-start
  55.9 6.8 %copy-start.3 = (f32[64,128]{1,0:T(8,128)S(1)}, f32[64,128]{1,0:T(8,128)}, u32[]{:S(2)}) copy-start(f32[64,128]{1,0:T(8,128)} %get-tuple-element.12) | copy-start | bytes 98308
  55.9 45.9 %all-to-all-start.1 = ((bf16[16,2,128,128]{3,2,1,0:T(8,128)(2,1)}), bf16[16,2,128,128]{3,2,1,0:T(8,128)(2,1)S(1)}, u32[]{:S(2)}, u32[]{:S(2)}) async-start(bf16[16,2,128,128]{3,2,1,0:T(8,128)(2,1)} %get-tuple-element.9), calls=%async_computation.1 | async-start | bytes 2097152 | tf_op jit(solution)/shard_map/all_to_all | solution.py:173

commit v11 on v10

--- a/solution.py
+++ b/solution.py
@@ -34,11 +34,18 @@
     return flat_rows.reshape(heads_here, BLOCK_LEN, table_width + 1).sum(axis=1)[:, :table_width]
 
 
-def split_kernel(query_ref, grad_ref, out_ref):
+def split_kernel(query_ref, grad_ref, out_ref, copy_sems):
+    copies = []
     for head in range(out_ref.shape[0]):
-        columns = slice(head * HEAD_DIM, (head + 1) * HEAD_DIM)
-        out_ref[head, 0] = query_ref[:, columns]
-        out_ref[head, 1] = grad_ref[:, columns]
+        columns = pl.ds(head * HEAD_DIM, HEAD_DIM)
+        for half, source in enumerate((query_ref, grad_ref)):
+            copy = pltpu.make_async_copy(
+                source.at[:, columns], out_ref.at[head, half], copy_sems.at[head, half]
+            )
+            copy.start()
+            copies.append(copy)
+    for copy in copies:
+        copy.wait()
 
 
 def attend_kernel(qd_ref, keys_ref, values_ref, keys_t_ref, values_t_ref, bias_ref, mask_ref, out_ref, key_out, value_out,
@@ -164,6 +171,9 @@
     score_scale = 1.0 / math.sqrt(HEAD_DIM)
     both_rows = pl.pallas_call(
         split_kernel,
+        in_specs=[pl.BlockSpec(memory_space=pl.ANY), pl.BlockSpec(memory_space=pl.ANY)],
+        out_specs=pl.BlockSpec(memory_space=pl.ANY),
+        scratch_shapes=[pltpu.SemaphoreType.DMA((heads_total, 2))],
         out_shape=jax.ShapeDtypeStruct((heads_total, 2, token_rows, HEAD_DIM), queries.dtype),
     )(queries.reshape(token_rows, full_width), cotangent.reshape(token_rows, full_width))
     both_heads = lax.all_to_all(both_rows, "enc", split_axis=0, concat_axis=0, tiled=True)

time: 105 us -> 136 us (1.30)
  Pallas kernels: 12.9 us -> 43.7 us
    pallas_call x1, Pallas kernels: 2.37 us -> 33.2 us  [local(): pl.pallas_call(split_kernel, in_specs=[pl.BlockSpec(memory_space=pl.ANY),...]
  transfers between devices with their start and end apart: 2 -> 2, of which waited for: 1 -> 1; matrix products, arithmetic and copies ran while one was open for 5% -> 4% of each run, Pallas kernels for 0% -> 0%
where the time goes in v11:
time: 136 us; the launch traced here: 135 us
  Pallas kernels  43.7 us (32%)
  blocking collectives  38.6 us (28%)
  starting transfers between devices  23.2 us (17%)
  waiting for transfers between devices  19 us (14%)
  local copies, waits for them, and re-layouts  9.93 us (7%)
    psum x2, blocking collectives, reduce_groups(): return lax.psum(lax.psum(part, 'seq'), 'dp')  38.6 us
    pallas_call x1, Pallas kernels, local(): pl.pallas_call(split_kernel, in_specs=[pl.BlockSpec(memory_space=pl.ANY),...  33.2 us
    all_to_all x1, waiting for transfers between devices, local(): lax.all_to_all(both_rows, 'enc', split_axis=0, concat_axis=0, tiled=True)  19 us
    all_to_all x1, starting transfers between devices, local(): lax.all_to_all(both_rows, 'enc', split_axis=0, concat_axis=0, tiled=True)  16.4 us
    pallas_call x1, Pallas kernels, attend_all(): pl.pallas_call(attend_kernel, grid=grid, in_specs=[pl.BlockSpec((seqs_ste...  10.5 us
    all_to_all x1, starting transfers between devices, local(): lax.all_to_all(both_out, 'enc', split_axis=0, concat_axis=0, tiled=True)  6.74 us
    unnamed x19, local copies, waits for them, and re-layouts  5.44 us
  transfers between devices with their start and end apart: 2, of which 1 were waited for; matrix products, arithmetic and copies ran while one was open for 4% of the time, Pallas kernels for 0%

profile of v11, /device:TPU:16, one launch (start us, length us, event | category | flops | bytes accessed | tf_op | source)
XLA Modules:
  0.0 135.1 jit_solution(649180380207583179)
XLA Ops:
  0.6 33.2 %shard_map.110 = bf16[16,2,128,128]{3,2,1,0:T(8,128)(2,1)} custom-call(bf16[128,2048]{1,0:T(8,128)(2,1)} %bitcast.33, bf16[128,2048]{1,0:T(8,128)(2,1)} %bitcast.34), custom_call_target="tpu_custom_call" | custom-call | tf_op jit(solution)/shard_map/pallas_call | solution.py:172
  33.8 16.4 %all-to-all-start = ((bf16[16,2,128,128]{3,2,1,0:T(8,128)(2,1)}), bf16[16,2,128,128]{3,2,1,0:T(8,128)(2,1)S(1)}, u32[]{:S(2)}, u32[]{:S(2)}) async-start(bf16[16,2,128,128]{3,2,1,0:T(8,128)(2,1)} %shard_map.110), calls=%async_computation | async-start | bytes 2097152 | tf_op jit(solution)/shard_map/all_to_all | solution.py:179
  50.3 0.1 copy.30
  50.3 0.1 lt.20
  50.4 0.6 copy-done.4
  51.0 0.1 copy.31
  51.1 0.1 copy.32
  51.3 0.6 copy-done.6
  51.9 0.1 broadcast_in_dim.21
  52.0 0.1 slice_reduce_fusion
  52.2 0.2 reshape.75
  52.4 0.1 broadcast_in_dim.22
  52.5 0.7 reshape_reshape.11.mask_ref
  53.3 0.8 copy.44
  54.1 0.2 copy-done.1
  54.2 0.8 copy.40
  55.1 0.1 copy-done.2
  55.2 0.8 copy.41
  56.0 19.0 %all-to-all-done.qd_ref = bf16[16,2,128,128]{3,2,1,0:T(8,128)(2,1)S(1)} async-done(((bf16[16,2,128,128]{3,2,1,0:T(8,128)(2,1)}), bf16[16,2,128,128]{3,2,1,0:T(8,128)(2,1)S(1)}, u32[]{:S(2)}, u32[]{:S(2)}) %all-to-all-start) | async-done | bytes 1048608 | tf_op jit(solution)/shard_map/all_to_all | solution.py:179
  75.0 1.0 copy-done
  76.0 10.5 %shard_map.111 = (bf16[16,2,128,128]{3,2,1,0:T(8,128)(2,1)}, bf16[1024,128]{1,0:T(8,128)(2,1)}, bf16[1024,128]{1,0:T(8,128)(2,1)}, f32[64,128]{1,0:T(8,128)}) custom-call(bf16[16,2,128,128]{3,2,1,0:T(8,128)(2,1)} %copy-done, bf16[1024,128]{1,0:T(8,128)(2,1)} %bitcast.25, bf16[1024,128]{1,0:T(8,128)(2,1)} %bitcast.27, bf16[128,1024]{1,0:T(8,128)(2,1)} %bitcast.30, ...), custom_call_target="tpu_custom_call" | custom-call | tf_op jit(solution)/shard_map/pallas_call | solution.py:122
  86.5 6.7 %all-to-all-start.1 = ((bf16[16,2,128,128]{3,2,1,0:T(8,128)(2,1)}), bf16[16,2,128,128]{3,2,1,0:T(8,128)(2,1)S(1)}, u32[]{:S(2)}, u32[]{:S(2)}) async-start(bf16[16,2,128,128]{3,2,1,0:T(8,128)(2,1)} %get-tuple-element.9), calls=%async_computation.1 | async-start | bytes 2097152 | tf_op jit(solution)/shard_map/all_to_all | solution.py:183
  93.3 0.1 pad.13
  93.4 0.3 reshape.78
  93.6 0.1 pad_reduce_fusion
  93.9 21.0 %psum.14 = f32[1,191]{1,0:T(1,128)S(1)} all-reduce(f32[1,191]{1,0:T(1,128)S(1)} %bitcast.37), channel_id=1, replica_groups=mesh['dp'=8,'seq'=8,'enc'=16] {'seq'}, use_global_device_ids=true, to_apply=%region_2.3 | all-reduce | flops 191 | bytes 1528 | tf_op jit(solution)/shard_map/psum | solution.py:156
  114.9 17.6 %psum.15 = f32[1,191]{1,0:T(1,128)} all-reduce(f32[1,191]{1,0:T(1,128)S(1)} %psum.14), channel_id=1, replica_groups=mesh['dp'=8,'seq'=8,'enc'=16] {'dp'}, use_global_device_ids=true, to_apply=%region_3.4 | all-reduce | flops 191 | bytes 1528 | tf_op jit(solution)/shard_map/psum | solution.py:156
  132.4 0.1 fusion.2
  132.5 0.3 copy.37
  132.8 1.0 copy.39
  133.9 0.3 copy.36
  134.1 1.0 copy.38
  (20 shorter events, 0.3 us)
Async XLA Ops:
  33.8 16.5 %copy-start.5 = (s32[16,2]{0,1:T(2,128)S(1)}, s32[16,2]{0,1:T(2,128)}, u32[]{:S(2)}) copy-start(s32[16,2]{0,1:T(2,128)} %param.11) | copy-start | bytes 388
  33.8 41.2 %all-to-all-start = ((bf16[16,2,128,128]{3,2,1,0:T(8,128)(2,1)}), bf16[16,2,128,128]{3,2,1,0:T(8,128)(2,1)S(1)}, u32[]{:S(2)}, u32[]{:S(2)}) async-start(bf16[16,2,128,128]{3,2,1,0:T(8,128)(2,1)} %shard_map.110), calls=%async_computation | async-start | bytes 2097152 | tf_op jit(solution)/shard_map/all_to_all | solution.py:179
  50.3 0.7 copy-start.4
  51.2 0.7 copy-start.6
  53.3 1.0 copy-start.1
  54.2 0.9 copy-start.2
  75.0 1.0 copy-start
  86.5 6.8 %copy-start.3 = (f32[64,128]{1,0:T(8,128)S(1)}, f32[64,128]{1,0:T(8,128)}, u32[]{:S(2)}) copy-start(f32[64,128]{1,0:T(8,128)} %get-tuple-element.12) | copy-start | bytes 98308
  86.5 45.9 %all-to-all-start.1 = ((bf16[16,2,128,128]{3,2,1,0:T(8,128)(2,1)}), bf16[16,2,128,128]{3,2,1,0:T(8,128)(2,1)S(1)}, u32[]{:S(2)}, u32[]{:S(2)}) async-start(bf16[16,2,128,128]{3,2,1,0:T(8,128)(2,1)} %get-tuple-element.9), calls=%async_computation.1 | async-start | bytes 2097152 | tf_op jit(solution)/shard_map/all_to_all | solution.py:183

commit v12 on v10

--- a/solution.py
+++ b/solution.py
@@ -162,8 +162,12 @@
     count_table = counts.reshape(-1)
     row_bias = bias_rows(rel_bias)
     score_scale = 1.0 / math.sqrt(HEAD_DIM)
+    split_rows = BLOCK_LEN
     both_rows = pl.pallas_call(
         split_kernel,
+        grid=(token_rows // split_rows,),
+        in_specs=[pl.BlockSpec((split_rows, full_width), lambda i: (i, 0))] * 2,
+        out_specs=pl.BlockSpec((heads_total, 2, split_rows, HEAD_DIM), lambda i: (0, 0, i, 0)),
         out_shape=jax.ShapeDtypeStruct((heads_total, 2, token_rows, HEAD_DIM), queries.dtype),
     )(queries.reshape(token_rows, full_width), cotangent.reshape(token_rows, full_width))
     both_heads = lax.all_to_all(both_rows, "enc", split_axis=0, concat_axis=0, tiled=True)

time: 105 us -> 105 us (level)
  no operation moved by 1% of the time
where the time goes in v12:
time: 105 us; the launch traced here: 104 us
  blocking collectives  38.5 us (37%)
  starting transfers between devices  23.3 us (22%)
  waiting for transfers between devices  19 us (18%)
  Pallas kernels  12.7 us (12%)
  local copies, waits for them, and re-layouts  9.93 us (9%)
    psum x2, blocking collectives, reduce_groups(): return lax.psum(lax.psum(part, 'seq'), 'dp')  38.5 us
    all_to_all x1, waiting for transfers between devices, local(): lax.all_to_all(both_rows, 'enc', split_axis=0, concat_axis=0, tiled=True)  19 us
    all_to_all x1, starting transfers between devices, local(): lax.all_to_all(both_rows, 'enc', split_axis=0, concat_axis=0, tiled=True)  16.6 us
    pallas_call x1, Pallas kernels, attend_all(): pl.pallas_call(attend_kernel, grid=grid, in_specs=[pl.BlockSpec((seqs_ste...  10.5 us
    all_to_all x1, starting transfers between devices, local(): lax.all_to_all(both_out, 'enc', split_axis=0, concat_axis=0, tiled=True)  6.75 us
    unnamed x19, local copies, waits for them, and re-layouts  5.44 us
    pallas_call x1, Pallas kernels, local(): pl.pallas_call(split_kernel, grid=(token_rows // split_rows,), in_specs=[...  2.14 us
  transfers between devices with their start and end apart: 2, of which 1 were waited for; matrix products, arithmetic and copies ran while one was open for 5% of the time, Pallas kernels for 0%

profile of v12, /device:TPU:16, one launch (start us, length us, event | category | flops | bytes accessed | tf_op | source)
XLA Modules:
  0.0 104.2 jit_solution(11474510795454120506)
XLA Ops:
  0.6 2.1 %shard_map.110 = bf16[16,2,128,128]{3,2,1,0:T(8,128)(2,1)} custom-call(bf16[128,2048]{1,0:T(8,128)(2,1)} %bitcast.33, bf16[128,2048]{1,0:T(8,128)(2,1)} %bitcast.34), custom_call_target="tpu_custom_call" | custom-call | tf_op jit(solution)/shard_map/pallas_call | solution.py:166
  2.8 16.6 %all-to-all-start = ((bf16[16,2,128,128]{3,2,1,0:T(8,128)(2,1)}), bf16[16,2,128,128]{3,2,1,0:T(8,128)(2,1)S(1)}, u32[]{:S(2)}, u32[]{:S(2)}) async-start(bf16[16,2,128,128]{3,2,1,0:T(8,128)(2,1)} %shard_map.110), calls=%async_computation | async-start | bytes 2097152 | tf_op jit(solution)/shard_map/all_to_all | solution.py:173
  19.3 0.1 copy.30
  19.4 0.1 lt.20
  19.5 0.6 copy-done.4
  20.1 0.1 copy.31
  20.2 0.1 copy.32
  20.4 0.6 copy-done.6
  21.0 0.1 broadcast_in_dim.21
  21.1 0.1 slice_reduce_fusion
  21.3 0.2 reshape.75
  21.5 0.1 broadcast_in_dim.22
  21.6 0.7 reshape_reshape.11.mask_ref
  22.4 0.8 copy.44
  23.2 0.2 copy-done.1
  23.3 0.8 copy.40
  24.2 0.1 copy-done.2
  24.3 0.8 copy.41
  25.1 19.0 %all-to-all-done.qd_ref = bf16[16,2,128,128]{3,2,1,0:T(8,128)(2,1)S(1)} async-done(((bf16[16,2,128,128]{3,2,1,0:T(8,128)(2,1)}), bf16[16,2,128,128]{3,2,1,0:T(8,128)(2,1)S(1)}, u32[]{:S(2)}, u32[]{:S(2)}) %all-to-all-start) | async-done | bytes 1048608 | tf_op jit(solution)/shard_map/all_to_all | solution.py:173
  44.1 1.0 copy-done
  45.1 10.5 %shard_map.111 = (bf16[16,2,128,128]{3,2,1,0:T(8,128)(2,1)}, bf16[1024,128]{1,0:T(8,128)(2,1)}, bf16[1024,128]{1,0:T(8,128)(2,1)}, f32[64,128]{1,0:T(8,128)}) custom-call(bf16[16,2,128,128]{3,2,1,0:T(8,128)(2,1)} %copy-done, bf16[1024,128]{1,0:T(8,128)(2,1)} %bitcast.25, bf16[1024,128]{1,0:T(8,128)(2,1)} %bitcast.27, bf16[128,1024]{1,0:T(8,128)(2,1)} %bitcast.30, ...), custom_call_target="tpu_custom_call" | custom-call | tf_op jit(solution)/shard_map/pallas_call | solution.py:115
  55.6 6.7 %all-to-all-start.1 = ((bf16[16,2,128,128]{3,2,1,0:T(8,128)(2,1)}), bf16[16,2,128,128]{3,2,1,0:T(8,128)(2,1)S(1)}, u32[]{:S(2)}, u32[]{:S(2)}) async-start(bf16[16,2,128,128]{3,2,1,0:T(8,128)(2,1)} %get-tuple-element.9), calls=%async_computation.1 | async-start | bytes 2097152 | tf_op jit(solution)/shard_map/all_to_all | solution.py:177
  62.4 0.1 pad.13
  62.5 0.3 reshape.78
  62.7 0.1 pad_reduce_fusion
  63.0 21.0 %psum.14 = f32[1,191]{1,0:T(1,128)S(1)} all-reduce(f32[1,191]{1,0:T(1,128)S(1)} %bitcast.37), channel_id=1, replica_groups=mesh['dp'=8,'seq'=8,'enc'=16] {'seq'}, use_global_device_ids=true, to_apply=%region_2.3 | all-reduce | flops 191 | bytes 1528 | tf_op jit(solution)/shard_map/psum | solution.py:149
  84.0 17.6 %psum.15 = f32[1,191]{1,0:T(1,128)} all-reduce(f32[1,191]{1,0:T(1,128)S(1)} %psum.14), channel_id=1, replica_groups=mesh['dp'=8,'seq'=8,'enc'=16] {'dp'}, use_global_device_ids=true, to_apply=%region_3.4 | all-reduce | flops 191 | bytes 1528 | tf_op jit(solution)/shard_map/psum | solution.py:149
  101.5 0.1 fusion.2
  101.6 0.3 copy.37
  101.9 1.0 copy.39
  102.9 0.3 copy.36
  103.2 1.0 copy.38
  (20 shorter events, 0.3 us)
Async XLA Ops:
  2.8 16.6 %copy-start.5 = (s32[16,2]{0,1:T(2,128)S(1)}, s32[16,2]{0,1:T(2,128)}, u32[]{:S(2)}) copy-start(s32[16,2]{0,1:T(2,128)} %param.11) | copy-start | bytes 388
  2.8 41.3 %all-to-all-start = ((bf16[16,2,128,128]{3,2,1,0:T(8,128)(2,1)}), bf16[16,2,128,128]{3,2,1,0:T(8,128)(2,1)S(1)}, u32[]{:S(2)}, u32[]{:S(2)}) async-start(bf16[16,2,128,128]{3,2,1,0:T(8,128)(2,1)} %shard_map.110), calls=%async_computation | async-start | bytes 2097152 | tf_op jit(solution)/shard_map/all_to_all | solution.py:173
  19.4 0.7 copy-start.4
  20.3 0.7 copy-start.6
  22.4 1.0 copy-start.1
  23.3 0.9 copy-start.2
  44.1 1.0 copy-start
  55.6 6.8 %copy-start.3 = (f32[64,128]{1,0:T(8,128)S(1)}, f32[64,128]{1,0:T(8,128)}, u32[]{:S(2)}) copy-start(f32[64,128]{1,0:T(8,128)} %get-tuple-element.12) | copy-start | bytes 98308
  55.6 45.9 %all-to-all-start.1 = ((bf16[16,2,128,128]{3,2,1,0:T(8,128)(2,1)}), bf16[16,2,128,128]{3,2,1,0:T(8,128)(2,1)S(1)}, u32[]{:S(2)}, u32[]{:S(2)}) async-start(bf16[16,2,128,128]{3,2,1,0:T(8,128)(2,1)} %get-tuple-element.9), calls=%async_computation.1 | async-start | bytes 2097152 | tf_op jit(solution)/shard_map/all_to_all | solution.py:177

commit v13 on v12

--- a/solution.py
+++ b/solution.py
@@ -162,7 +162,7 @@
     count_table = counts.reshape(-1)
     row_bias = bias_rows(rel_bias)
     score_scale = 1.0 / math.sqrt(HEAD_DIM)
-    split_rows = BLOCK_LEN
+    split_rows = BLOCK_LEN // 2
     both_rows = pl.pallas_call(
         split_kernel,
         grid=(token_rows // split_rows,),

time: 105 us -> 106 us (level)
  Pallas kernels: 12.7 us -> 14 us
    pallas_call x1, Pallas kernels: 2.14 us -> 3.51 us  [local(): pl.pallas_call(split_kernel, grid=(token_rows // split_rows,), in_specs=[...]
where the time goes in v13:
time: 106 us
  blocking collectives  38.5 us (36%)
  starting transfers between devices  23.3 us (22%)
  waiting for transfers between devices  19 us (18%)
  Pallas kernels  14 us (13%)
  local copies, waits for them, and re-layouts  9.93 us (9%)
    psum x2, blocking collectives, reduce_groups(): return lax.psum(lax.psum(part, 'seq'), 'dp')  38.5 us
    all_to_all x1, waiting for transfers between devices, local(): lax.all_to_all(both_rows, 'enc', split_axis=0, concat_axis=0, tiled=True)  19 us
    all_to_all x1, starting transfers between devices, local(): lax.all_to_all(both_rows, 'enc', split_axis=0, concat_axis=0, tiled=True)  16.6 us
    pallas_call x1, Pallas kernels, attend_all(): pl.pallas_call(attend_kernel, grid=grid, in_specs=[pl.BlockSpec((seqs_ste...  10.5 us
    all_to_all x1, starting transfers between devices, local(): lax.all_to_all(both_out, 'enc', split_axis=0, concat_axis=0, tiled=True)  6.76 us
    unnamed x19, local copies, waits for them, and re-layouts  5.44 us
    pallas_call x1, Pallas kernels, local(): pl.pallas_call(split_kernel, grid=(token_rows // split_rows,), in_specs=[...  3.51 us
  transfers between devices with their start and end apart: 2, of which 1 were waited for; matrix products, arithmetic and copies ran while one was open for 5% of the time, Pallas kernels for 0%

profile of v13, /device:TPU:16, one launch (start us, length us, event | category | flops | bytes accessed | tf_op | source)
XLA Modules:
  0.0 105.6 jit_solution(3019186699181236422)
XLA Ops:
  0.6 3.5 %shard_map.110 = bf16[16,2,128,128]{3,2,1,0:T(8,128)(2,1)} custom-call(bf16[128,2048]{1,0:T(8,128)(2,1)} %bitcast.33, bf16[128,2048]{1,0:T(8,128)(2,1)} %bitcast.34), custom_call_target="tpu_custom_call" | custom-call | tf_op jit(solution)/shard_map/pallas_call | solution.py:166
  4.1 16.6 %all-to-all-start = ((bf16[16,2,128,128]{3,2,1,0:T(8,128)(2,1)}), bf16[16,2,128,128]{3,2,1,0:T(8,128)(2,1)S(1)}, u32[]{:S(2)}, u32[]{:S(2)}) async-start(bf16[16,2,128,128]{3,2,1,0:T(8,128)(2,1)} %shard_map.110), calls=%async_computation | async-start | bytes 2097152 | tf_op jit(solution)/shard_map/all_to_all | solution.py:173
  20.7 0.1 copy.30
  20.8 0.1 lt.20
  20.9 0.6 copy-done.4
  21.5 0.1 copy.31
  21.6 0.1 copy.32
  21.8 0.6 copy-done.6
  22.4 0.1 broadcast_in_dim.21
  22.5 0.1 slice_reduce_fusion
  22.6 0.2 reshape.75
  22.8 0.1 broadcast_in_dim.22
  22.9 0.7 reshape_reshape.11.mask_ref
  23.8 0.8 copy.44
  24.5 0.2 copy-done.1
  24.7 0.8 copy.40
  25.6 0.1 copy-done.2
  25.6 0.8 copy.41
  26.5 19.0 %all-to-all-done.qd_ref = bf16[16,2,128,128]{3,2,1,0:T(8,128)(2,1)S(1)} async-done(((bf16[16,2,128,128]{3,2,1,0:T(8,128)(2,1)}), bf16[16,2,128,128]{3,2,1,0:T(8,128)(2,1)S(1)}, u32[]{:S(2)}, u32[]{:S(2)}) %all-to-all-start) | async-done | bytes 1048608 | tf_op jit(solution)/shard_map/all_to_all | solution.py:173
  45.5 1.0 copy-done
  46.5 10.5 %shard_map.111 = (bf16[16,2,128,128]{3,2,1,0:T(8,128)(2,1)}, bf16[1024,128]{1,0:T(8,128)(2,1)}, bf16[1024,128]{1,0:T(8,128)(2,1)}, f32[64,128]{1,0:T(8,128)}) custom-call(bf16[16,2,128,128]{3,2,1,0:T(8,128)(2,1)} %copy-done, bf16[1024,128]{1,0:T(8,128)(2,1)} %bitcast.25, bf16[1024,128]{1,0:T(8,128)(2,1)} %bitcast.27, bf16[128,1024]{1,0:T(8,128)(2,1)} %bitcast.30, ...), custom_call_target="tpu_custom_call" | custom-call | tf_op jit(solution)/shard_map/pallas_call | solution.py:115
  57.0 6.8 %all-to-all-start.1 = ((bf16[16,2,128,128]{3,2,1,0:T(8,128)(2,1)}), bf16[16,2,128,128]{3,2,1,0:T(8,128)(2,1)S(1)}, u32[]{:S(2)}, u32[]{:S(2)}) async-start(bf16[16,2,128,128]{3,2,1,0:T(8,128)(2,1)} %get-tuple-element.9), calls=%async_computation.1 | async-start | bytes 2097152 | tf_op jit(solution)/shard_map/all_to_all | solution.py:177
  63.8 0.1 pad.13
  63.8 0.3 reshape.78
  64.1 0.1 pad_reduce_fusion
  64.3 21.0 %psum.14 = f32[1,191]{1,0:T(1,128)S(1)} all-reduce(f32[1,191]{1,0:T(1,128)S(1)} %bitcast.37), channel_id=1, replica_groups=mesh['dp'=8,'seq'=8,'enc'=16] {'seq'}, use_global_device_ids=true, to_apply=%region_2.3 | all-reduce | flops 191 | bytes 1528 | tf_op jit(solution)/shard_map/psum | solution.py:149
  85.3 17.6 %psum.15 = f32[1,191]{1,0:T(1,128)} all-reduce(f32[1,191]{1,0:T(1,128)S(1)} %psum.14), channel_id=1, replica_groups=mesh['dp'=8,'seq'=8,'enc'=16] {'dp'}, use_global_device_ids=true, to_apply=%region_3.4 | all-reduce | flops 191 | bytes 1528 | tf_op jit(solution)/shard_map/psum | solution.py:149
  102.9 0.1 fusion.2
  103.0 0.3 copy.37
  103.3 1.0 copy.39
  104.3 0.3 copy.36
  104.6 1.0 copy.38
  (20 shorter events, 0.3 us)
Async XLA Ops:
  4.1 16.6 %copy-start.5 = (s32[16,2]{0,1:T(2,128)S(1)}, s32[16,2]{0,1:T(2,128)}, u32[]{:S(2)}) copy-start(s32[16,2]{0,1:T(2,128)} %param.11) | copy-start | bytes 388
  4.1 41.3 %all-to-all-start = ((bf16[16,2,128,128]{3,2,1,0:T(8,128)(2,1)}), bf16[16,2,128,128]{3,2,1,0:T(8,128)(2,1)S(1)}, u32[]{:S(2)}, u32[]{:S(2)}) async-start(bf16[16,2,128,128]{3,2,1,0:T(8,128)(2,1)} %shard_map.110), calls=%async_computation | async-start | bytes 2097152 | tf_op jit(solution)/shard_map/all_to_all | solution.py:173
  20.8 0.7 copy-start.4
  21.7 0.7 copy-start.6
  23.7 1.0 copy-start.1
  24.7 0.9 copy-start.2
  45.5 1.0 copy-start
  57.0 6.8 %copy-start.3 = (f32[64,128]{1,0:T(8,128)S(1)}, f32[64,128]{1,0:T(8,128)}, u32[]{:S(2)}) copy-start(f32[64,128]{1,0:T(8,128)} %get-tuple-element.12) | copy-start | bytes 98308
  57.0 45.9 %all-to-all-start.1 = ((bf16[16,2,128,128]{3,2,1,0:T(8,128)(2,1)}), bf16[16,2,128,128]{3,2,1,0:T(8,128)(2,1)S(1)}, u32[]{:S(2)}, u32[]{:S(2)}) async-start(bf16[16,2,128,128]{3,2,1,0:T(8,128)(2,1)} %get-tuple-element.9), calls=%async_computation.1 | async-start | bytes 2097152 | tf_op jit(solution)/shard_map/all_to_all | solution.py:177
